TPU v7x, 32 devices: a whole 2x2x4 slice. The times are simulated.
32 devices in a mesh: section: 2 (over core), latent: 4 (over z), tok: 4 (over y, x).
Axes of the slice: x: 2, y: 2, z: 4, core: 2. Of those that a mesh axis runs over, the one named last changes fastest.
Arguments:
- acts: bfloat16 [2, 256, 8192], P('section', 'latent', 'tok'), may hold values from -6 to 6
- enc_weight: bfloat16 [2, 8192, 32768], P('section', 'tok', 'latent'), may hold values from -0.046875 to 0.046875
- enc_bias: float32 [32768], P('latent'), may hold values from -3 to 3
- dec_weight: bfloat16 [32768, 2, 8192], P('latent', 'section', 'tok'), may hold values from -0.15625 to 0.15625
- dec_bias: float32 [2, 8192], P('section', 'tok'), may hold values from -3 to 3
- active_blocks: int32 [2, 32], replicated, may hold values from 0 to 255, as said below
- block_counts: int32 [2], replicated, may hold values from 16 to 32
Outputs:
- rebuilt: bfloat16 [2, 256, 8192], P('section', 'latent', 'tok')
Inputs may be any that keep to these rules, and one draw needn't show every extreme that they name: `active_blocks`: within a tile the 32 listed ids are distinct; entries past the tile's count are ignored.
All inputs are finite; a program needn't handle non-finite values.
Results may differ from a plain program's by a relative error of at most 0.0048.
Values may be sent and summed in bfloat16 or wider, within the bound.
No kernel may reach another device: no remote copies, remote signals or barrier semaphores. Data moves between devices by JAX's collectives and lax.ppermute only.
A program may use at most 128 MiB of HBM per device.

v0:
```python
import jax
import jax.numpy as jnp
from jax import lax
from jax.sharding import PartitionSpec as P

BLOCK = 128
TILE = 128


def shards(acts, enc_weight, enc_bias, dec_weight, dec_bias, active_blocks, block_counts):
    local_enc = enc_weight[0]
    preact = jnp.dot(
        lax.all_gather(acts, "latent", axis=1, tiled=True)[0],
        local_enc,
        preferred_element_type=jnp.float32,
    )
    blocks_local = local_enc.shape[1] // BLOCK
    first_block = lax.axis_index("latent") * blocks_local
    block_ids = first_block + jnp.arange(blocks_local, dtype=jnp.int32)
    slot_ids = jnp.arange(active_blocks.shape[1], dtype=jnp.int32)
    in_list = slot_ids[None, :] < block_counts[:, None]
    matches = (active_blocks[:, :, None] == block_ids[None, None, :]) & in_list[:, :, None]
    tile_mask = jnp.any(matches, axis=1).astype(jnp.float32)
    tile_numbers = jnp.arange(tile_mask.shape[0], dtype=jnp.int32)
    shared = lax.psum_scatter(preact, ("section", "tok"), scatter_dimension=0, tiled=True)
    row_begin = lax.axis_index(("section", "tok")) * shared.shape[0]
    row_total = shared.shape[0]
    tile_of_row = (row_begin + jnp.arange(row_total, dtype=jnp.int32)) // TILE
    picker = (tile_of_row[:, None] == tile_numbers[None, :]).astype(jnp.float32)
    row_mask = jnp.dot(picker, tile_mask, preferred_element_type=jnp.float32)
    latent_mask = jnp.repeat(row_mask, BLOCK, axis=1)
    latent_codes = lax.all_gather(
        (jax.nn.relu(shared + enc_bias[None, :]) * latent_mask).astype(jnp.bfloat16),
        ("section", "tok"),
        axis=0,
        tiled=True,
    )
    local_dec = dec_weight[:, 0, :]
    rebuilt = lax.psum_scatter(
        jnp.dot(latent_codes, local_dec, preferred_element_type=jnp.float32),
        "latent",
        scatter_dimension=0,
        tiled=True,
    )
    return (rebuilt + dec_bias).astype(jnp.bfloat16)[None]


def solution(mesh):
    placed = (
        P("section", "latent", "tok"),
        P("section", "tok", "latent"),
        P("latent"),
        P("latent", "section", "tok"),
        P("section", "tok"),
        P(),
        P(),
    )
    return jax.shard_map(
        shards, mesh=mesh, in_specs=placed, out_specs=P("section", "latent", "tok"), check_vma=False
    )
```

profile of v0, /device:TPU:0, one launch (start us, length us, event | category | flops | bytes accessed | tf_op | source)
XLA Modules:
  0.0 237.4 jit_solution(14967038014017623821)
XLA Ops:
  6.5 0.0 all-gather.3.cloned.1.call-start
  6.5 0.7 all-gather.3.cloned.1.call-update
  7.3 0.0 copy-start.3
  7.3 0.0 copy-start.2
  7.3 0.0 copy-start
  7.3 0.0 reduce-scatter.3.cloned.1.call-start
  7.3 32.3 %all-gather.3.cloned.1.call-done = bf16[1,256,2048]{2,1,0:T(8,128)(2,1)} async-done(((bf16[1,64,2048]{2,1,0:T(8,128)(2,1)}), bf16[1,256,2048]{2,1,0:T(8,128)(2,1)}) %all-gather.3.cloned.1.call-update) | async-done | bytes 1048592 | tf_op jit(solution)/shard_map/all_gather | solution.py:13
  39.6 17.3 %fusion.2 = f32[256,8192]{1,0:T(8,128)} fusion(bf16[1,2048,8192]{2,1,0:T(8,128)(2,1)} %param.8, bf16[1,256,2048]{2,1,0:T(8,128)(2,1)} %all-gather.3.cloned.1.call-done), kind=kOutput, calls=%fused_computation.2 | convolution fusion | flops 8589934592 | bytes 42991616 | tf_op jit(solution)/shard_map/dot_general | solution.py:12
  56.9 0.0 reduce-scatter.3.cloned.1.call-update
  56.9 0.0 all-gather.5.cloned.1.call-start
  57.0 0.0 copy-done.3
  57.0 0.1 iota_compare_fusion.2
  57.1 0.0 copy-done.2
  57.1 0.1 and_reduce_fusion
  57.2 0.2 fusion.7
  57.4 70.5 %reduce-scatter.3.cloned.1.call-done = f32[32,8192]{1,0:T(8,128)} async-done(((f32[256,8192]{1,0:T(8,128)}), f32[32,8192]{1,0:T(8,128)}) %reduce-scatter.3.cloned.1.call-update) | async-done | bytes 1048592 | tf_op jit(solution)/shard_map/reduce_scatter | solution.py:25
  127.9 0.3 broadcast_in_dim.4
  128.2 0.0 copy-done
  128.2 2.7 %fusion.4 = bf16[32,8192]{1,0:T(8,128)(2,1)} fusion(f32[4,8,64,128]{3,2,1,0:T(8,128)S(1)} %bitcast.19, f32[32,8192]{1,0:T(8,128)} %reduce-scatter.3.cloned.1.call-done, f32[8192]{0:T(1024)S(1)} %copy-done), kind=kLoop, calls=%fused_computation.5 | loop fusion | flops 1048576 | bytes 2654208 | tf_op jit(solution)/shard_map/convert_element_type | solution.py:33
  130.9 0.0 copy-start.1
  130.9 0.0 all-gather.5.cloned.1.call-update
  130.9 0.0 reduce-scatter.5.cloned.1.call-start
  131.0 36.8 %all-gather.5.cloned.1.call-done = bf16[256,8192]{1,0:T(8,128)(2,1)} async-done(((bf16[32,8192]{1,0:T(8,128)(2,1)}), bf16[256,8192]{1,0:T(8,128)(2,1)}) %all-gather.5.cloned.1.call-update) | async-done | bytes 4194320 | tf_op jit(solution)/shard_map/all_gather | solution.py:32
  167.8 17.2 %fusion = f32[256,2048]{1,0:T(8,128)} fusion(bf16[256,8192]{1,0:T(8,128)(2,1)} %all-gather.5.cloned.1.call-done, bf16[8192,1,2048]{2,0,1:T(8,128)(2,1)} %param.10), kind=kOutput, calls=%fused_computation | convolution fusion | flops 8589934592 | bytes 39845888 | tf_op jit(solution)/shard_map/dot_general | solution.py:40
  185.0 0.0 reduce-scatter.5.cloned.1.call-update
  185.0 44.0 %reduce-scatter.5.cloned.1.call-done = f32[64,2048]{1,0:T(8,128)} async-done(((f32[256,2048]{1,0:T(8,128)}), f32[64,2048]{1,0:T(8,128)}) %reduce-scatter.5.cloned.1.call-update) | async-done | bytes 524304 | tf_op jit(solution)/shard_map/reduce_scatter | solution.py:39
  229.1 0.0 copy-done.1
  229.1 1.8 fusion.6
  (2 shorter events, 0.0 us)
Async XLA Ops:
  6.5 33.1 %all-gather.3.cloned.1.call-start = ((), (), s32[]{:S(2)}) async-start(), calls=%async_computation.2 | async-start | bytes 1310720 | tf_op jit(solution)/shard_map/all_gather | solution.py:13
  7.3 49.7 %copy-start.3 = (s32[2]{0:T(128)S(1)}, s32[2]{0:T(128)}, u32[]{:S(2)}) copy-start(s32[2]{0:T(128)} %param.13) | copy-start | bytes 28
  7.3 49.8 %copy-start.2 = (s32[2,32]{1,0:T(2,128)S(1)}, s32[2,32]{1,0:T(2,128)}, u32[]{:S(2)}) copy-start(s32[2,32]{1,0:T(2,128)} %param.12) | copy-start | bytes 772
  7.3 120.9 %copy-start = (f32[8192]{0:T(1024)S(1)}, f32[8192]{0:T(1024)}, u32[]{:S(2)}) copy-start(f32[8192]{0:T(1024)} %param.9) | copy-start | bytes 98308
  7.3 120.6 %reduce-scatter.3.cloned.1.call-start = ((), (), s32[]{:S(2)}) async-start(), calls=%async_computation.3 | async-start | bytes 9437184 | tf_op jit(solution)/shard_map/reduce_scatter | solution.py:25
  56.9 110.9 %all-gather.5.cloned.1.call-start = ((), (), s32[]{:S(2)}) async-start(), calls=%async_computation.4 | async-start | bytes 4718592 | tf_op jit(solution)/shard_map/all_gather | solution.py:32
  130.9 98.2 %copy-start.1 = (f32[1,2048]{1,0:T(1,128)S(1)}, f32[1,2048]{1,0:T(1,128)}, u32[]{:S(2)}) copy-start(f32[1,2048]{1,0:T(1,128)} %param.11) | copy-start | bytes 24580
  130.9 98.1 %reduce-scatter.5.cloned.1.call-start = ((), (), s32[]{:S(2)}) async-start(), calls=%async_computation.5 | async-start | bytes 2621440 | tf_op jit(solution)/shard_map/reduce_scatter | solution.py:39
Sparse Core Ops, SparseCore 0:
  8.9 30.6 all-gather.2
  57.0 70.7 reduce-scatter.2
  131.0 36.6 all-gather.4
  185.1 43.8 reduce-scatter.4
where the time goes:
time: 238 us; the launch traced here: 237 us
  waiting for transfers between devices  184 us (77%)
  matrix products  34.7 us (15%)
  between operations  13.2 us (6%)
  other arithmetic  4.67 us (2%)
    reduce_scatter x1, waiting for transfers between devices, shards(): lax.psum_scatter(preact, ('section', 'tok'), scatter_dimension=0, tiled=T...  70.5 us
    reduce_scatter x1, waiting for transfers between devices, shards(): lax.psum_scatter(jnp.dot(latent_codes, local_dec, preferred_element_type=...  44 us
    all_gather x1, waiting for transfers between devices, shards(): lax.all_gather((jax.nn.relu(shared + enc_bias[None, :]) * latent_mask).as...  36.8 us
    all_gather x1, waiting for transfers between devices, shards(): lax.all_gather(acts, 'latent', axis=1, tiled=True)[0]  32.3 us
    dot_general x1, matrix products, shards(): jnp.dot(lax.all_gather(acts, 'latent', axis=1, tiled=True)[0], local_enc,...  17.3 us
    dot_general x1, matrix products, shards(): jnp.dot(latent_codes, local_dec, preferred_element_type=jnp.float32)  17.2 us
  transfers between devices with their start and end apart: 4, of which 4 were waited for; matrix products, arithmetic and copies ran while one was open for 0% of the time, Pallas kernels for 0%

commit v1 on v0

v1 whole, which is shorter than its diff:
```python
import jax
import jax.numpy as jnp
from jax import lax
from jax.sharding import PartitionSpec as P

BLOCK = 128
TILE = 128


def slot_table(active_blocks, block_counts, first_block, blocks_local, slots):
    listed = active_blocks.shape[1]
    slot_ids = jnp.arange(listed, dtype=jnp.int32)
    local = active_blocks - first_block
    valid = (slot_ids[None, :] < block_counts[:, None]) & (local >= 0) & (local < blocks_local)
    order = jnp.argsort(jnp.logical_not(valid).astype(jnp.int32), axis=1, stable=True)[:, :slots]
    picked_valid = jnp.take_along_axis(valid, order, axis=1)
    picked = jnp.where(picked_valid, jnp.take_along_axis(local, order, axis=1), 0)
    return picked, picked_valid


def shards(acts, enc_weight, enc_bias, dec_weight, dec_bias, active_blocks, block_counts):
    local_enc = enc_weight[0]
    tokens_all = lax.all_gather(acts, "latent", axis=1, tiled=True)[0]
    preact = jnp.dot(tokens_all, local_enc, preferred_element_type=jnp.float32)
    n_tok, n_lat = preact.shape
    tiles = n_tok // TILE
    blocks_local = n_lat // BLOCK
    slots = min(active_blocks.shape[1], blocks_local)
    first_block = lax.axis_index("latent") * blocks_local
    picked, picked_valid = slot_table(active_blocks, block_counts, first_block, blocks_local, slots)

    tiled_pre = preact.reshape(tiles, TILE, blocks_local, BLOCK)
    compact = jax.vmap(lambda p, i: p[:, i, :])(tiled_pre, picked)
    shared = lax.psum_scatter(compact, ("section", "tok"), scatter_dimension=1, tiled=True)
    bias_slots = enc_bias.reshape(blocks_local, BLOCK)[picked]
    keep = picked_valid.astype(jnp.float32)[:, None, :, None]
    codes_part = (jax.nn.relu(shared + bias_slots[:, None, :, :]) * keep).astype(jnp.bfloat16)
    codes_compact = lax.all_gather(codes_part, ("section", "tok"), axis=1, tiled=True)

    dense = jnp.zeros((tiles, TILE, blocks_local, BLOCK), jnp.bfloat16)
    dense = jax.vmap(lambda d, i, c: d.at[:, i, :].add(c))(dense, picked, codes_compact)
    latent_codes = dense.reshape(n_tok, n_lat)

    local_dec = dec_weight[:, 0, :]
    rebuilt = lax.psum_scatter(
        jnp.dot(latent_codes, local_dec, preferred_element_type=jnp.float32),
        "latent",
        scatter_dimension=0,
        tiled=True,
    )
    return (rebuilt + dec_bias).astype(jnp.bfloat16)[None]


def solution(mesh):
    placed = (
        P("section", "latent", "tok"),
        P("section", "tok", "latent"),
        P("latent"),
        P("latent", "section", "tok"),
        P("section", "tok"),
        P(),
        P(),
    )
    return jax.shard_map(
        shards, mesh=mesh, in_specs=placed, out_specs=P("section", "latent", "tok"), check_vma=False
    )
```

time: 238 us -> 265 us (1.11)
  local copies, waits for them, and re-layouts: 0.34 us -> 61.5 us
  waiting for transfers between devices: 184 us -> 126 us
  other arithmetic: 4.67 us -> 20 us
  matrix products: 34.7 us -> 41 us
    dot_general x0 -> x1, local copies, waits for them, and re-layouts: none -> 44.5 us  [shards(): preact = jnp.dot(tokens_all, local_enc, preferred_element_type=jnp.float32)]
    all_gather x2, waiting for transfers between devices: 69.1 us -> 28.1 us  [the longest x1 28 us: shards(): lax.all_gather(codes_part, ('section', 'tok'), axis=1, tiled=True)]
    reduce_scatter x1, waiting for transfers between devices: 70.5 us -> 53.4 us  [shards(): lax.psum_scatter(compact, ('section', 'tok'), scatter_dimension=1, tiled=...]
    scatter-add x0 -> x3, other arithmetic: none -> 14.8 us  [shards(): d.at[:, i, :].add(c)]
    gather x0 -> x7, local copies, waits for them, and re-layouts: none -> 8.74 us  [the longest x1 6.13 us: shards(): compact = jax.vmap(lambda p, i: p[:, i, :])(tiled_pre, picked)]
    dot_general x1, matrix products: 17.2 us -> 22.6 us  [shards(): jnp.dot(latent_codes, local_dec, preferred_element_type=jnp.float32)]
    scatter-add x0 -> x3, local copies, waits for them, and re-layouts: none -> 5.05 us  [shards(): d.at[:, i, :].add(c)]
    broadcast_in_dim x1, local copies, waits for them, and re-layouts: 0.32 us -> 2.98 us  [shards(): dense = jnp.zeros((tiles, TILE, blocks_local, BLOCK), jnp.bfloat16)]
  transfers between devices with their start and end apart: 4 -> 4, of which waited for: 4 -> 3; matrix products, arithmetic and copies ran while one was open for 0% -> 19% of each run, Pallas kernels for 0% -> 0%
where the time goes in v1:
time: 265 us; the launch traced here: 262 us
  waiting for transfers between devices  126 us (48%)
  local copies, waits for them, and re-layouts  61.5 us (23%)
  matrix products  41 us (15%)
  other arithmetic  20 us (8%)
  between operations  13.2 us (5%)
    reduce_scatter x1, waiting for transfers between devices, shards(): lax.psum_scatter(compact, ('section', 'tok'), scatter_dimension=1, tiled=...  53.4 us
    dot_general x1, local copies, waits for them, and re-layouts, shards(): preact = jnp.dot(tokens_all, local_enc, preferred_element_type=jnp.float32)  44.5 us
    reduce_scatter x1, waiting for transfers between devices, shards(): lax.psum_scatter(jnp.dot(latent_codes, local_dec, preferred_element_type=...  44.2 us
    all_gather x1, waiting for transfers between devices, shards(): lax.all_gather(codes_part, ('section', 'tok'), axis=1, tiled=True)  28 us
    dot_general x1, matrix products, shards(): jnp.dot(latent_codes, local_dec, preferred_element_type=jnp.float32)  22.6 us
    dot_general x1, matrix products, shards(): preact = jnp.dot(tokens_all, local_enc, preferred_element_type=jnp.float32)  18.4 us
    scatter-add x3, other arithmetic, shards(): d.at[:, i, :].add(c)  14.8 us
    gather x1, local copies, waits for them, and re-layouts, shards(): compact = jax.vmap(lambda p, i: p[:, i, :])(tiled_pre, picked)  6.13 us
  transfers between devices with their start and end apart: 4, of which 3 were waited for; matrix products, arithmetic and copies ran while one was open for 19% of the time, Pallas kernels for 0%

profile of v1, /device:TPU:0, one launch (start us, length us, event | category | flops | bytes accessed | tf_op | source)
XLA Modules:
  0.0 262.4 jit_solution(8201835750939643065)
XLA Ops:
  6.5 0.7 all-gather.3.cloned.1.call-update
  7.3 0.0 reduce-scatter.3.cloned.1.call-start
  7.3 0.8 not_convert_fusion
  8.1 0.1 copy.9
  8.2 0.8 sort.17
  9.0 0.1 copy.10
  9.1 0.1 reshape.47
  9.2 0.9 gather_fusion.1
  10.0 0.1 reshape.50
  10.1 0.9 gather_fusion.2
  11.0 0.1 reshape.56
  11.1 0.1 reshape.59
  11.2 44.5 %copy.16 = bf16[8192,2048]{1,0:T(8,128)(2,1)} copy(bf16[8192,2048]{0,1:T(8,128)(2,1)} %bitcast.46) | data formatting | bytes 67108864 | tf_op jit(solution)/shard_map/dot_general | solution.py:24
  55.7 18.4 %fusion.9 = f32[2,128,64,128]{3,1,2,0:T(8,128)} fusion(bf16[2,128,2048,1]{2,1,3,0:T(8,128)(2,1)} %bitcast.53, bf16[64,128,2048,1]{2,1,0,3:T(8,128)(2,1)} %bitcast.47), kind=kOutput, calls=%fused_computation.27 | convolution fusion | flops 8589934592 | bytes 42991616 | tf_op jit(solution)/shard_map/dot_general | solution.py:24
  74.1 6.1 %gather_fusion.3 = f32[64,128,128]{2,1,0:T(8,128)} fusion(f32[2,128,64,128]{3,1,2,0:T(8,128)} %fusion.9, s32[64]{0:T(128)S(1)} %reshape.59), kind=kCustom, calls=%fused_computation.3 | custom fusion | bytes 8389120 | tf_op jit(solution)/shard_map/vmap()/gather | solution.py:33
  80.2 0.0 reduce-scatter.3.cloned.1.call-update
  80.3 0.0 all-gather.5.cloned.1.call-start
  80.3 0.1 reshape.41
  80.4 0.6 gather_fusion
  81.0 53.4 %reduce-scatter.3.cloned.1.call-done = f32[2,16,32,128]{3,1,2,0:T(8,128)} async-done(((f32[2,128,32,128]{3,1,2,0:T(8,128)}), f32[2,16,32,128]{3,1,2,0:T(8,128)}) %reduce-scatter.3.cloned.1.call-update) | async-done | bytes 524304 | tf_op jit(solution)/shard_map/reduce_scatter | solution.py:34
  134.4 1.9 multiply_convert_fusion
  136.3 0.0 all-gather.5.cloned.1.call-update
  136.3 0.2 reduce-scatter.5.cloned.1.call-start
  136.5 0.1 reshape.65
  136.6 28.0 %all-gather.5.cloned.1.call-done = bf16[2,128,32,128]{3,1,2,0:T(8,128)(2,1)} async-done(((bf16[2,16,32,128]{3,1,2,0:T(8,128)(2,1)}), bf16[2,128,32,128]{3,1,2,0:T(8,128)(2,1)}) %all-gather.5.cloned.1.call-update) | async-done | bytes 2097168 | tf_op jit(solution)/shard_map/all_gather | solution.py:38
  164.7 3.0 %broadcast_in_dim.14 = bf16[2,128,64,128]{3,1,2,0:T(8,128)(2,1)} broadcast(bf16[]{:T(256)} %constant.21.clone.1), dimensions={} | broadcast | bytes 4194306 | tf_op jit(solution)/shard_map/broadcast_in_dim | solution.py:40
  167.7 14.8 %scatter_fusion = bf16[2,128,64,128]{3,1,2,0:T(8,128)(2,1)} fusion(bf16[2,128,64,128]{3,1,2,0:T(8,128)(2,1)} %broadcast_in_dim.14, s32[64]{0:T(128)S(1)} %reshape.65, bf16[64,128,128]{2,1,0:T(8,128)(2,1)S(1)} %bitcast.50), kind=kCustom, calls=%fused_computation.4 | custom fusion | flops 1048576 | bytes 6291968 | tf_op jit(solution)/shard_map/vmap()/scatter-add | solution.py:41
  182.4 4.9 %copy.14 = bf16[2,128,64,128]{3,2,1,0:T(8,128)(2,1)S(1)} copy(bf16[2,128,64,128]{3,1,2,0:T(8,128)(2,1)} %scatter_fusion) | data formatting | bytes 8388608 | tf_op jit(solution)/shard_map/vmap()/scatter-add | solution.py:41
  187.3 22.6 %fusion = f32[256,2048]{1,0:T(8,128)} fusion(bf16[8192,1,2048]{2,0,1:T(8,128)(2,1)} %param.10, bf16[32,8,64,128]{3,2,1,0:T(8,128)(2,1)S(1)} %bitcast.49), kind=kOutput, calls=%fused_computation.5 | convolution fusion | flops 8589934592 | bytes 39845888 | tf_op jit(solution)/shard_map/dot_general | solution.py:46
  209.9 0.0 reduce-scatter.5.cloned.1.call-update
  210.0 44.2 %reduce-scatter.5.cloned.1.call-done = f32[64,2048]{1,0:T(8,128)} async-done(((f32[256,2048]{1,0:T(8,128)}), f32[64,2048]{1,0:T(8,128)}) %reduce-scatter.5.cloned.1.call-update) | async-done | bytes 524304 | tf_op jit(solution)/shard_map/reduce_scatter | solution.py:45
  254.1 1.8 fusion.4
  (14 shorter events, 0.1 us)
Async XLA Ops:
  6.5 73.9 %copy-start = (f32[8192]{0:T(1024)S(1)}, f32[8192]{0:T(1024)}, u32[]{:S(2)}) copy-start(f32[8192]{0:T(1024)} %param.9) | copy-start | bytes 98308
  6.5 49.1 %all-gather.3.cloned.1.call-start = ((), (), s32[]{:S(2)}) async-start(), calls=%async_computation.2 | async-start | bytes 1310720 | tf_op jit(solution)/shard_map/all_gather | solution.py:23
  7.3 127.1 %reduce-scatter.3.cloned.1.call-start = ((), (), s32[]{:S(2)}) async-start(), calls=%async_computation.3 | async-start | bytes 4718592 | tf_op jit(solution)/shard_map/reduce_scatter | solution.py:34
  80.3 84.4 %all-gather.5.cloned.1.call-start = ((), (), s32[]{:S(2)}) async-start(), calls=%async_computation.4 | async-start | bytes 2359296 | tf_op jit(solution)/shard_map/all_gather | solution.py:38
  136.3 117.8 %reduce-scatter.5.cloned.1.call-start = ((), (), s32[]{:S(2)}) async-start(), calls=%async_computation.5 | async-start | bytes 2621440 | tf_op jit(solution)/shard_map/reduce_scatter | solution.py:45
  164.7 3.0 %copy-start.1 = (bf16[2,128,32,128]{3,1,2,0:T(8,128)(2,1)S(1)}, bf16[2,128,32,128]{3,1,2,0:T(8,128)(2,1)}, u32[]{:S(2)}) copy-start(bf16[2,128,32,128]{3,1,2,0:T(8,128)(2,1)} %all-gather.5.cloned.1.call-done) | copy-start | bytes 6291460
  187.3 66.8 %copy-start.2 = (f32[1,2048]{1,0:T(1,128)S(1)}, f32[1,2048]{1,0:T(1,128)}, u32[]{:S(2)}) copy-start(f32[1,2048]{1,0:T(1,128)} %param.11) | copy-start | bytes 24580
Sparse Core Ops, SparseCore 0:
  8.9 30.6 all-gather.2
  80.4 53.9 reduce-scatter.2
  136.4 28.1 all-gather.4
  210.1 44.0 reduce-scatter.4

commit v2 on v1

v2 whole, which is shorter than its diff:
```python
import functools

import jax
import jax.numpy as jnp
from jax import lax
from jax.experimental import pallas as pl
from jax.experimental.pallas import tpu as pltpu
from jax.sharding import PartitionSpec as P

BLOCK = 128
TILE = 128


def slot_table(active_blocks, block_counts, first_block, blocks_local, slots):
    listed = active_blocks.shape[1]
    slot_ids = jnp.arange(listed, dtype=jnp.int32)
    local = active_blocks - first_block
    valid = (slot_ids[None, :] < block_counts[:, None]) & (local >= 0) & (local < blocks_local)
    order = jnp.argsort(jnp.logical_not(valid).astype(jnp.int32), axis=1, stable=True)[:, :slots]
    picked_valid = jnp.take_along_axis(valid, order, axis=1)
    picked = jnp.where(picked_valid, jnp.take_along_axis(local, order, axis=1), 0)
    flat_valid = picked_valid.reshape(-1)
    flat_order = jnp.argsort(jnp.logical_not(flat_valid).astype(jnp.int32), stable=True).astype(jnp.int32)
    flat_blocks = picked.reshape(-1)[flat_order]
    count = jnp.sum(flat_valid.astype(jnp.int32)).reshape(1)
    return picked_valid, count, flat_order, flat_blocks


def encode_kernel(n_ref, slot_ref, blk_ref, acts_ref, enc_hbm, out_ref, buf, sem):
    slots = out_ref.shape[1]
    out_ref[...] = jnp.zeros(out_ref.shape, out_ref.dtype)
    n = n_ref[0]

    def copy(i, slot):
        col = pl.multiple_of(blk_ref[i] * BLOCK, BLOCK)
        return pltpu.make_async_copy(enc_hbm.at[:, pl.ds(col, BLOCK)], buf.at[slot], sem.at[slot])

    @pl.when(n > 0)
    def _():
        copy(0, 0).start()

    def body(i, carry):
        slot = i % 2
        copy(i, slot).wait()

        @pl.when(i + 1 < n)
        def _():
            copy(i + 1, 1 - slot).start()

        s = slot_ref[i]
        t = s // slots
        k = s % slots
        rows = acts_ref[pl.ds(pl.multiple_of(t * TILE, TILE), TILE), :]
        out_ref[t, k] = jnp.dot(rows, buf[slot], preferred_element_type=jnp.float32)
        return carry

    lax.fori_loop(0, n, body, 0)


def decode_kernel(n_ref, slot_ref, blk_ref, codes_ref, dec_hbm, out_ref, buf, sem):
    slots = codes_ref.shape[1]
    out_ref[...] = jnp.zeros(out_ref.shape, out_ref.dtype)
    n = n_ref[0]

    def copy(i, slot):
        row = pl.multiple_of(blk_ref[i] * BLOCK, BLOCK)
        return pltpu.make_async_copy(dec_hbm.at[pl.ds(row, BLOCK), :], buf.at[slot], sem.at[slot])

    @pl.when(n > 0)
    def _():
        copy(0, 0).start()

    def body(i, carry):
        slot = i % 2
        copy(i, slot).wait()

        @pl.when(i + 1 < n)
        def _():
            copy(i + 1, 1 - slot).start()

        s = slot_ref[i]
        t = s // slots
        k = s % slots
        rows = pl.ds(pl.multiple_of(t * TILE, TILE), TILE)
        out_ref[rows, :] += jnp.dot(codes_ref[t, k], buf[slot], preferred_element_type=jnp.float32)
        return carry

    lax.fori_loop(0, n, body, 0)


def sparse_call(kernel, out_shape, buf_shape, count, flat_order, flat_blocks, dense, weight, flops, nbytes):
    smem = pl.BlockSpec(memory_space=pltpu.SMEM)
    return pl.pallas_call(
        kernel,
        out_shape=out_shape,
        in_specs=[smem, smem, smem, pl.BlockSpec(memory_space=pltpu.VMEM), pl.BlockSpec(memory_space=pl.ANY)],
        out_specs=pl.BlockSpec(memory_space=pltpu.VMEM),
        scratch_shapes=[pltpu.VMEM(buf_shape, weight.dtype), pltpu.SemaphoreType.DMA((2,))],
        cost_estimate=pl.CostEstimate(flops=flops, bytes_accessed=nbytes, transcendentals=0),
    )(count, flat_order, flat_blocks, dense, weight)


def shards(acts, enc_weight, enc_bias, dec_weight, dec_bias, active_blocks, block_counts):
    local_enc = enc_weight[0]
    local_dec = dec_weight[:, 0, :]
    width, n_lat = local_enc.shape
    tokens_all = lax.all_gather(acts, "latent", axis=1, tiled=True)[0]
    n_tok = tokens_all.shape[0]
    tiles = n_tok // TILE
    blocks_local = n_lat // BLOCK
    slots = min(active_blocks.shape[1], blocks_local)
    first_block = lax.axis_index("latent") * blocks_local
    picked_valid, count, flat_order, flat_blocks = slot_table(
        active_blocks, block_counts, first_block, blocks_local, slots
    )
    pairs = tiles * slots

    compact = sparse_call(
        encode_kernel,
        jax.ShapeDtypeStruct((tiles, slots, TILE, BLOCK), jnp.float32),
        (2, width, BLOCK),
        count, flat_order, flat_blocks, tokens_all, local_enc,
        2 * pairs * TILE * width * BLOCK, pairs * (width * BLOCK * 2 + TILE * BLOCK * 4),
    )
    shared = lax.psum_scatter(compact, ("section", "tok"), scatter_dimension=2, tiled=True)
    bias_slots = enc_bias.reshape(blocks_local, BLOCK)
    slot_blocks = jnp.zeros((tiles * slots,), jnp.int32).at[flat_order].set(flat_blocks).reshape(tiles, slots)
    bias_slots = bias_slots[slot_blocks]
    codes_part = jnp.where(
        picked_valid[:, :, None, None], jax.nn.relu(shared + bias_slots[:, :, None, :]), 0.0
    ).astype(jnp.bfloat16)
    codes = lax.all_gather(codes_part, ("section", "tok"), axis=2, tiled=True)

    partial = sparse_call(
        decode_kernel,
        jax.ShapeDtypeStruct((n_tok, local_dec.shape[1]), jnp.float32),
        (2, BLOCK, local_dec.shape[1]),
        count, flat_order, flat_blocks, codes, local_dec,
        2 * pairs * TILE * BLOCK * local_dec.shape[1], pairs * BLOCK * local_dec.shape[1] * 2,
    )
    rebuilt = lax.psum_scatter(partial, "latent", scatter_dimension=0, tiled=True)
    return (rebuilt + dec_bias).astype(jnp.bfloat16)[None]


def solution(mesh):
    placed = (
        P("section", "latent", "tok"),
        P("section", "tok", "latent"),
        P("latent"),
        P("latent", "section", "tok"),
        P("section", "tok"),
        P(),
        P(),
    )
    return jax.shard_map(
        shards, mesh=mesh, in_specs=placed, out_specs=P("section", "latent", "tok"), check_vma=False
    )
```

time: 265 us -> 217 us (0.82); the launches traced: 262 us -> 221 us
  local copies, waits for them, and re-layouts: 61.5 us -> 5.38 us
  matrix products: 41 us -> 0 us
  waiting for transfers between devices: 126 us -> 167 us
  Pallas kernels: 0 us -> 26.7 us
  other arithmetic: 20 us -> 7.99 us
    dot_general x1 -> x0, local copies, waits for them, and re-layouts: 44.5 us -> none  [shards(): preact = jnp.dot(tokens_all, local_enc, preferred_element_type=jnp.float32)]
    dot_general x2 -> x0, matrix products: 41 us -> none  [the longest x1 22.6 us: shards(): jnp.dot(latent_codes, local_dec, preferred_element_type=jnp.float32)]
    pallas_call x0 -> x2, Pallas kernels: none -> 26.7 us  [sparse_call(): pl.pallas_call(kernel, out_shape=out_shape, in_specs=[smem, smem, smem, p...]
    all_gather x1, waiting for transfers between devices: 0.01 us -> 24.3 us  [shards(): tokens_all = lax.all_gather(acts, 'latent', axis=1, tiled=True)[0]]
    reduce_scatter x2, waiting for transfers between devices: 97.6 us -> 114 us  [the longest x1 59.6 us: shards(): lax.psum_scatter(compact, ('section', 'tok'), scatter_dimension=2, tiled=...]
    scatter-add x3 -> x0, other arithmetic: 14.8 us -> none  [shards(): d.at[:, i, :].add(c)]
    scatter-add x3 -> x0, local copies, waits for them, and re-layouts: 5.05 us -> none  [shards(): d.at[:, i, :].add(c)]
    gather x2, local copies, waits for them, and re-layouts: 6.73 us -> 1.96 us  [the longest x1 1.36 us: slot_table(): flat_blocks = picked.reshape(-1)[flat_order]]
  transfers between devices with their start and end apart: 4 -> 4, of which waited for: 3 -> 4; matrix products, arithmetic and copies ran while one was open for 19% -> 4% of each run, Pallas kernels for 0% -> 0%
where the time goes in v2:
time: 217 us; the launch traced here: 221 us
  waiting for transfers between devices  167 us (77%)
  Pallas kernels  26.7 us (12%)
  between operations  13.2 us (6%)
  other arithmetic  7.99 us (4%)
  local copies, waits for them, and re-layouts  5.38 us (2%)
    reduce_scatter x1, waiting for transfers between devices, shards(): lax.psum_scatter(compact, ('section', 'tok'), scatter_dimension=2, tiled=...  59.6 us
    reduce_scatter x1, waiting for transfers between devices, shards(): lax.psum_scatter(partial, 'latent', scatter_dimension=0, tiled=True)  54.4 us
    all_gather x1, waiting for transfers between devices, shards(): codes = lax.all_gather(codes_part, ('section', 'tok'), axis=2, tiled=True)  28.3 us
    pallas_call x2, Pallas kernels, sparse_call(): pl.pallas_call(kernel, out_shape=out_shape, in_specs=[smem, smem, smem, p...  26.7 us
    all_gather x1, waiting for transfers between devices, shards(): tokens_all = lax.all_gather(acts, 'latent', axis=1, tiled=True)[0]  24.3 us
  transfers between devices with their start and end apart: 4, of which 4 were waited for; matrix products, arithmetic and copies ran while one was open for 4% of the time, Pallas kernels for 0%

profile of v2, /device:TPU:0, one launch (start us, length us, event | category | flops | bytes accessed | tf_op | source)
XLA Modules:
  0.0 220.8 jit_solution(6268797568394521928)
XLA Ops:
  6.5 0.7 all-gather.3.cloned.1.call-update
  7.3 0.0 reduce-scatter.3.cloned.1.call-start
  7.3 0.8 not_convert_fusion.1
  8.1 0.1 copy.8
  8.2 0.8 sort.34
  9.0 0.1 copy.9
  9.1 0.1 reshape.97
  9.2 0.9 gather_fusion.2
  10.0 0.1 reshape.100
  10.1 0.9 gather_fusion.3
  11.0 0.1 reshape.106
  11.1 0.1 reshape.80
  11.2 0.1 select_n.53
  11.3 2.0 sort.35
  13.3 1.4 gather_fusion
  14.7 0.7 convert_reduce_fusion
  15.3 24.3 %all-gather.3.cloned.1.call-done = bf16[1,256,2048]{2,1,0:T(8,128)(2,1)} async-done(((bf16[1,64,2048]{2,1,0:T(8,128)(2,1)}), bf16[1,256,2048]{2,1,0:T(8,128)(2,1)}) %all-gather.3.cloned.1.call-update) | async-done | bytes 1048592 | tf_op jit(solution)/shard_map/all_gather | solution.py:107
  39.6 13.5 %shard_map.73 = f32[2,32,128,128]{3,2,1,0:T(8,128)} custom-call(s32[1]{0:T(128)} %bitcast.1.n_ref, s32[64]{0:T(128)} %copy-done.3, s32[64]{0:T(128)} %gather_fusion, bf16[256,2048]{1,0:T(8,128)(2,1)} %bitcast.18, bf16[2048,8192]{1,0:T(8,128)(2,1)} %bitcast.16), custom_call_target="tpu_custom_call" | custom-call | flops 4294967296 | bytes 37748736 | tf_op jit(solution)/shard_map/pallas_call | solution.py:93
  53.1 0.0 reduce-scatter.3.cloned.1.call-update
  53.1 0.0 all-gather.5.cloned.1.call-start
  53.1 0.9 scatter_custom_fusion
  54.1 0.1 reshape.79
  54.1 0.1 reshape.91
  54.2 0.6 gather_fusion.1
  54.8 59.6 %reduce-scatter.3.cloned.1.call-done = f32[2,32,16,128]{3,2,1,0:T(8,128)} async-done(((f32[2,32,128,128]{3,2,1,0:T(8,128)}), f32[2,32,16,128]{3,2,1,0:T(8,128)}) %reduce-scatter.3.cloned.1.call-update) | async-done | bytes 524304 | tf_op jit(solution)/shard_map/reduce_scatter | solution.py:125
  114.5 1.9 select_convert_fusion
  116.4 0.0 reduce-scatter.5.cloned.1.call-start
  116.4 28.3 %all-gather.5.cloned.1.call-done.codes_ref = bf16[2,32,128,128]{3,2,1,0:T(8,128)(2,1)} async-done(((bf16[2,32,16,128]{3,2,1,0:T(8,128)(2,1)}), bf16[2,32,128,128]{3,2,1,0:T(8,128)(2,1)}) %all-gather.5.cloned.1.call-update) | async-done | bytes 2097168 | tf_op jit(solution)/shard_map/all_gather | solution.py:132
  144.7 13.3 %shard_map.74 = f32[256,2048]{1,0:T(8,128)} custom-call(s32[1]{0:T(128)} %bitcast.1.n_ref, s32[64]{0:T(128)} %copy-done.3, s32[64]{0:T(128)} %gather_fusion, bf16[2,32,128,128]{3,2,1,0:T(8,128)(2,1)} %all-gather.5.cloned.1.call-done.codes_ref, bf16[8192,2048]{1,0:T(8,128)(2,1)} %bitcast.17), custom_call_target="tpu_custom_call" | custom-call | flops 4294967296 | bytes 33554432 | tf_op jit(solution)/shard_map/pallas_call | solution.py:93
  158.0 0.0 reduce-scatter.5.cloned.1.call-update
  158.0 54.4 %reduce-scatter.5.cloned.1.call-done = f32[64,2048]{1,0:T(8,128)} async-done(((f32[256,2048]{1,0:T(8,128)}), f32[64,2048]{1,0:T(8,128)}) %reduce-scatter.5.cloned.1.call-update) | async-done | bytes 524304 | tf_op jit(solution)/shard_map/reduce_scatter | solution.py:141
  212.4 1.8 fusion
  (19 shorter events, 0.1 us)
Async XLA Ops:
  6.5 47.7 %copy-start = (f32[8192]{0:T(1024)S(1)}, f32[8192]{0:T(1024)}, u32[]{:S(2)}) copy-start(f32[8192]{0:T(1024)} %param.9) | copy-start | bytes 98308
  6.5 33.1 %all-gather.3.cloned.1.call-start = ((), (), s32[]{:S(2)}) async-start(), calls=%async_computation.2 | async-start | bytes 1310720 | tf_op jit(solution)/shard_map/all_gather | solution.py:107
  7.3 107.2 %reduce-scatter.3.cloned.1.call-start = ((), (), s32[]{:S(2)}) async-start(), calls=%async_computation.3 | async-start | bytes 4718592 | tf_op jit(solution)/shard_map/reduce_scatter | solution.py:125
  13.3 26.3 %copy-start.3 = (s32[64]{0:T(128)}, s32[64]{0:T(128)S(1)}, u32[]{:S(2)}) copy-start(s32[64]{0:T(128)S(1)} %get-tuple-element.8.slot_ref) | copy-start | bytes 772
  53.1 91.6 %all-gather.5.cloned.1.call-start = ((), (), s32[]{:S(2)}) async-start(), calls=%async_computation.4 | async-start | bytes 2359296 | tf_op jit(solution)/shard_map/all_gather | solution.py:132
  116.4 96.1 %reduce-scatter.5.cloned.1.call-start = ((), (), s32[]{:S(2)}) async-start(), calls=%async_computation.5 | async-start | bytes 2621440 | tf_op jit(solution)/shard_map/reduce_scatter | solution.py:141
  144.7 67.7 %copy-start.2 = (f32[1,2048]{1,0:T(1,128)S(1)}, f32[1,2048]{1,0:T(1,128)}, u32[]{:S(2)}) copy-start(f32[1,2048]{1,0:T(1,128)} %param.11) | copy-start | bytes 24580
  144.7 69.5 %copy-start.1 = (f32[8192]{0:T(1024)S(1)}, f32[8192]{0:T(1024)}, u32[]{:S(2)}) copy-start(f32[8192]{0:T(1024)} %param.9) | copy-start | bytes 98308
Sparse Core Ops, SparseCore 0:
  8.9 30.6 all-gather.2
  53.2 61.1 reduce-scatter.2
  116.5 28.1 all-gather.4
  158.1 54.2 reduce-scatter.4

commit v3 on v2

--- a/solution.py
+++ b/solution.py
@@ -26,66 +26,64 @@
     return picked_valid, count, flat_order, flat_blocks
 
 
-def encode_kernel(n_ref, slot_ref, blk_ref, acts_ref, enc_hbm, out_ref, buf, sem):
-    slots = out_ref.shape[1]
-    out_ref[...] = jnp.zeros(out_ref.shape, out_ref.dtype)
-    n = n_ref[0]
+DEPTH = 6
 
+
+def weight_stream(n, blk_ref, source, buf, sem, compute):
     def copy(i, slot):
-        col = pl.multiple_of(blk_ref[i] * BLOCK, BLOCK)
-        return pltpu.make_async_copy(enc_hbm.at[:, pl.ds(col, BLOCK)], buf.at[slot], sem.at[slot])
+        return pltpu.make_async_copy(source(blk_ref[i]), buf.at[slot], sem.at[slot])
 
-    @pl.when(n > 0)
-    def _():
-        copy(0, 0).start()
+    for j in range(DEPTH):
+        @pl.when(j < n)
+        def _():
+            copy(j, j).start()
 
     def body(i, carry):
-        slot = i % 2
+        slot = i % DEPTH
         copy(i, slot).wait()
+        compute(i, buf.at[slot])
 
-        @pl.when(i + 1 < n)
+        @pl.when(i + DEPTH < n)
         def _():
-            copy(i + 1, 1 - slot).start()
+            copy(i + DEPTH, slot).start()
 
-        s = slot_ref[i]
-        t = s // slots
-        k = s % slots
-        rows = acts_ref[pl.ds(pl.multiple_of(t * TILE, TILE), TILE), :]
-        out_ref[t, k] = jnp.dot(rows, buf[slot], preferred_element_type=jnp.float32)
         return carry
 
     lax.fori_loop(0, n, body, 0)
 
 
+def encode_kernel(n_ref, slot_ref, blk_ref, acts_ref, enc_hbm, out_ref, buf, sem):
+    slots = out_ref.shape[1]
+    out_ref[...] = jnp.zeros(out_ref.shape, out_ref.dtype)
+
+    def source(b):
+        return enc_hbm.at[:, pl.ds(pl.multiple_of(b * BLOCK, BLOCK), BLOCK)]
+
+    def compute(i, block):
+        s = slot_ref[i]
+        t = s // slots
+        k = s % slots
+        rows = acts_ref[pl.ds(pl.multiple_of(t * TILE, TILE), TILE), :]
+        out_ref[t, k] = jnp.dot(rows, block[...], preferred_element_type=jnp.float32)
+
+    weight_stream(n_ref[0], blk_ref, source, buf, sem, compute)
+
+
 def decode_kernel(n_ref, slot_ref, blk_ref, codes_ref, dec_hbm, out_ref, buf, sem):
     slots = codes_ref.shape[1]
     out_ref[...] = jnp.zeros(out_ref.shape, out_ref.dtype)
-    n = n_ref[0]
 
-    def copy(i, slot):
-        row = pl.multiple_of(blk_ref[i] * BLOCK, BLOCK)
-        return pltpu.make_async_copy(dec_hbm.at[pl.ds(row, BLOCK), :], buf.at[slot], sem.at[slot])
+    def source(b):
+        return dec_hbm.at[pl.ds(pl.multiple_of(b * BLOCK, BLOCK), BLOCK), :]
 
-    @pl.when(n > 0)
-    def _():
-        copy(0, 0).start()
-
-    def body(i, carry):
-        slot = i % 2
-        copy(i, slot).wait()
-
-        @pl.when(i + 1 < n)
-        def _():
-            copy(i + 1, 1 - slot).start()
-
+    def compute(i, block):
         s = slot_ref[i]
         t = s // slots
         k = s % slots
         rows = pl.ds(pl.multiple_of(t * TILE, TILE), TILE)
-        out_ref[rows, :] += jnp.dot(codes_ref[t, k], buf[slot], preferred_element_type=jnp.float32)
-        return carry
+        out_ref[rows, :] += jnp.dot(codes_ref[t, k], block[...], preferred_element_type=jnp.float32)
 
-    lax.fori_loop(0, n, body, 0)
+    weight_stream(n_ref[0], blk_ref, source, buf, sem, compute)
 
 
 def sparse_call(kernel, out_shape, buf_shape, count, flat_order, flat_blocks, dense, weight, flops, nbytes):
@@ -95,7 +93,7 @@
         out_shape=out_shape,
         in_specs=[smem, smem, smem, pl.BlockSpec(memory_space=pltpu.VMEM), pl.BlockSpec(memory_space=pl.ANY)],
         out_specs=pl.BlockSpec(memory_space=pltpu.VMEM),
-        scratch_shapes=[pltpu.VMEM(buf_shape, weight.dtype), pltpu.SemaphoreType.DMA((2,))],
+        scratch_shapes=[pltpu.VMEM((DEPTH,) + buf_shape, weight.dtype), pltpu.SemaphoreType.DMA((DEPTH,))],
         cost_estimate=pl.CostEstimate(flops=flops, bytes_accessed=nbytes, transcendentals=0),
     )(count, flat_order, flat_blocks, dense, weight)
 
@@ -118,7 +116,7 @@
     compact = sparse_call(
         encode_kernel,
         jax.ShapeDtypeStruct((tiles, slots, TILE, BLOCK), jnp.float32),
-        (2, width, BLOCK),
+        (width, BLOCK),
         count, flat_order, flat_blocks, tokens_all, local_enc,
         2 * pairs * TILE * width * BLOCK, pairs * (width * BLOCK * 2 + TILE * BLOCK * 4),
     )
@@ -134,7 +132,7 @@
     partial = sparse_call(
         decode_kernel,
         jax.ShapeDtypeStruct((n_tok, local_dec.shape[1]), jnp.float32),
-        (2, BLOCK, local_dec.shape[1]),
+        (BLOCK, local_dec.shape[1]),
         count, flat_order, flat_blocks, codes, local_dec,
         2 * pairs * TILE * BLOCK * local_dec.shape[1], pairs * BLOCK * local_dec.shape[1] * 2,
     )

time: 217 us -> 191 us (0.88); the launches traced: 221 us -> 191 us
  waiting for transfers between devices: 167 us -> 143 us
  Pallas kernels: 26.7 us -> 20.7 us
    reduce_scatter x1, waiting for transfers between devices: 54.4 us -> 42.3 us  [shards(): lax.psum_scatter(partial, 'latent', scatter_dimension=0, tiled=True)]
    reduce_scatter x1, waiting for transfers between devices: 59.6 us -> 47.9 us  [shards(): lax.psum_scatter(compact, ('section', 'tok'), scatter_dimension=2, tiled=...]
    pallas_call x2, Pallas kernels: 26.7 us -> 20.7 us  [sparse_call(): pl.pallas_call(kernel, out_shape=out_shape, in_specs=[smem, smem, smem, p...]
  transfers between devices with their start and end apart: 4 -> 4, of which waited for: 4 -> 4; matrix products, arithmetic and copies ran while one was open for 4% -> 5% of each run, Pallas kernels for 0% -> 0%
where the time goes in v3:
time: 191 us
  waiting for transfers between devices  143 us (75%)
  Pallas kernels  20.7 us (11%)
  between operations  13.2 us (7%)
  other arithmetic  7.99 us (4%)
  local copies, waits for them, and re-layouts  5.38 us (3%)
    reduce_scatter x1, waiting for transfers between devices, shards(): lax.psum_scatter(compact, ('section', 'tok'), scatter_dimension=2, tiled=...  47.9 us
    reduce_scatter x1, waiting for transfers between devices, shards(): lax.psum_scatter(partial, 'latent', scatter_dimension=0, tiled=True)  42.3 us
    all_gather x1, waiting for transfers between devices, shards(): codes = lax.all_gather(codes_part, ('section', 'tok'), axis=2, tiled=True)  28.3 us
    all_gather x1, waiting for transfers between devices, shards(): tokens_all = lax.all_gather(acts, 'latent', axis=1, tiled=True)[0]  24.3 us
    pallas_call x2, Pallas kernels, sparse_call(): pl.pallas_call(kernel, out_shape=out_shape, in_specs=[smem, smem, smem, p...  20.7 us
  transfers between devices with their start and end apart: 4, of which 4 were waited for; matrix products, arithmetic and copies ran while one was open for 5% of the time, Pallas kernels for 0%

profile of v3, /device:TPU:0, one launch (start us, length us, event | category | flops | bytes accessed | tf_op | source)
XLA Modules:
  0.0 190.8 jit_solution(4484719783383636681)
XLA Ops:
  6.5 0.7 all-gather.3.cloned.1.call-update
  7.3 0.0 reduce-scatter.3.cloned.1.call-start
  7.3 0.8 not_convert_fusion.1
  8.1 0.1 copy.8
  8.2 0.8 sort.34
  9.0 0.1 copy.9
  9.1 0.1 reshape.97
  9.2 0.9 gather_fusion.2
  10.0 0.1 reshape.100
  10.1 0.9 gather_fusion.3
  11.0 0.1 reshape.106
  11.1 0.1 reshape.80
  11.2 0.1 select_n.53
  11.3 2.0 %sort.35 = (s32[64]{0:T(128)}, s32[64]{0:T(128)S(1)}) sort(s32[64]{0:T(128)S(1)} %reshape.80, s32[64]{0:T(128)S(1)} %iota.16), dimensions={0}, to_apply=%region_2.3 | sort | flops 384 | bytes 1024 | tf_op jit(solution)/shard_map/jit(argsort)/sort | solution.py:23
  13.3 1.4 gather_fusion
  14.7 0.7 convert_reduce_fusion
  15.3 24.3 %all-gather.3.cloned.1.call-done = bf16[1,256,2048]{2,1,0:T(8,128)(2,1)} async-done(((bf16[1,64,2048]{2,1,0:T(8,128)(2,1)}), bf16[1,256,2048]{2,1,0:T(8,128)(2,1)}) %all-gather.3.cloned.1.call-update) | async-done | bytes 1048592 | tf_op jit(solution)/shard_map/all_gather | solution.py:105
  39.6 10.5 %shard_map.73 = f32[2,32,128,128]{3,2,1,0:T(8,128)} custom-call(s32[1]{0:T(128)} %bitcast.1.n_ref, s32[64]{0:T(128)} %copy-done.3, s32[64]{0:T(128)} %gather_fusion, bf16[256,2048]{1,0:T(8,128)(2,1)} %bitcast.18, bf16[2048,8192]{1,0:T(8,128)(2,1)} %bitcast.16), custom_call_target="tpu_custom_call" | custom-call | flops 4294967296 | bytes 37748736 | tf_op jit(solution)/shard_map/pallas_call | solution.py:91
  50.1 0.0 reduce-scatter.3.cloned.1.call-update
  50.1 0.0 all-gather.5.cloned.1.call-start
  50.1 0.9 scatter_custom_fusion
  51.1 0.1 reshape.79
  51.1 0.1 reshape.91
  51.2 0.6 gather_fusion.1
  51.8 47.9 %reduce-scatter.3.cloned.1.call-done = f32[2,32,16,128]{3,2,1,0:T(8,128)} async-done(((f32[2,32,128,128]{3,2,1,0:T(8,128)}), f32[2,32,16,128]{3,2,1,0:T(8,128)}) %reduce-scatter.3.cloned.1.call-update) | async-done | bytes 524304 | tf_op jit(solution)/shard_map/reduce_scatter | solution.py:123
  99.7 1.9 select_convert_fusion
  101.6 0.0 reduce-scatter.5.cloned.1.call-start
  101.7 28.3 %all-gather.5.cloned.1.call-done.codes_ref = bf16[2,32,128,128]{3,2,1,0:T(8,128)(2,1)} async-done(((bf16[2,32,16,128]{3,2,1,0:T(8,128)(2,1)}), bf16[2,32,128,128]{3,2,1,0:T(8,128)(2,1)}) %all-gather.5.cloned.1.call-update) | async-done | bytes 2097168 | tf_op jit(solution)/shard_map/all_gather | solution.py:130
  130.0 10.2 %shard_map.74 = f32[256,2048]{1,0:T(8,128)} custom-call(s32[1]{0:T(128)} %bitcast.1.n_ref, s32[64]{0:T(128)} %copy-done.3, s32[64]{0:T(128)} %gather_fusion, bf16[2,32,128,128]{3,2,1,0:T(8,128)(2,1)} %all-gather.5.cloned.1.call-done.codes_ref, bf16[8192,2048]{1,0:T(8,128)(2,1)} %bitcast.17), custom_call_target="tpu_custom_call" | custom-call | flops 4294967296 | bytes 33554432 | tf_op jit(solution)/shard_map/pallas_call | solution.py:91
  140.2 0.0 reduce-scatter.5.cloned.1.call-update
  140.2 42.3 %reduce-scatter.5.cloned.1.call-done = f32[64,2048]{1,0:T(8,128)} async-done(((f32[256,2048]{1,0:T(8,128)}), f32[64,2048]{1,0:T(8,128)}) %reduce-scatter.5.cloned.1.call-update) | async-done | bytes 524304 | tf_op jit(solution)/shard_map/reduce_scatter | solution.py:139
  182.5 1.8 fusion
  (19 shorter events, 0.1 us)
Async XLA Ops:
  6.5 44.7 %copy-start = (f32[8192]{0:T(1024)S(1)}, f32[8192]{0:T(1024)}, u32[]{:S(2)}) copy-start(f32[8192]{0:T(1024)} %param.9) | copy-start | bytes 98308
  6.5 33.1 %all-gather.3.cloned.1.call-start = ((), (), s32[]{:S(2)}) async-start(), calls=%async_computation.2 | async-start | bytes 1310720 | tf_op jit(solution)/shard_map/all_gather | solution.py:105
  7.3 92.4 %reduce-scatter.3.cloned.1.call-start = ((), (), s32[]{:S(2)}) async-start(), calls=%async_computation.3 | async-start | bytes 4718592 | tf_op jit(solution)/shard_map/reduce_scatter | solution.py:123
  13.3 26.3 %copy-start.3 = (s32[64]{0:T(128)}, s32[64]{0:T(128)S(1)}, u32[]{:S(2)}) copy-start(s32[64]{0:T(128)S(1)} %get-tuple-element.8.slot_ref) | copy-start | bytes 772
  50.1 79.9 %all-gather.5.cloned.1.call-start = ((), (), s32[]{:S(2)}) async-start(), calls=%async_computation.4 | async-start | bytes 2359296 | tf_op jit(solution)/shard_map/all_gather | solution.py:130
  101.6 80.9 %reduce-scatter.5.cloned.1.call-start = ((), (), s32[]{:S(2)}) async-start(), calls=%async_computation.5 | async-start | bytes 2621440 | tf_op jit(solution)/shard_map/reduce_scatter | solution.py:139
  130.0 52.5 %copy-start.2 = (f32[1,2048]{1,0:T(1,128)S(1)}, f32[1,2048]{1,0:T(1,128)}, u32[]{:S(2)}) copy-start(f32[1,2048]{1,0:T(1,128)} %param.11) | copy-start | bytes 24580
  130.0 54.3 %copy-start.1 = (f32[8192]{0:T(1024)S(1)}, f32[8192]{0:T(1024)}, u32[]{:S(2)}) copy-start(f32[8192]{0:T(1024)} %param.9) | copy-start | bytes 98308
Sparse Core Ops, SparseCore 0:
  8.9 30.6 all-gather.2
  50.2 49.4 reduce-scatter.2
  101.7 28.1 all-gather.4
  140.4 42.0 reduce-scatter.4

commit v4 on v3

--- a/solution.py
+++ b/solution.py
@@ -98,11 +98,55 @@
     )(count, flat_order, flat_blocks, dense, weight)
 
 
+LINE_MAX = 4
+
+
+def line_pairs(n, k, rightward):
+    return [(i, i + k) if rightward else (i + k, i) for i in range(n - k)]
+
+
+def line_gather(x, axis):
+    n = lax.axis_size(axis)
+    if n > LINE_MAX:
+        return lax.all_gather(x, axis, axis=0, tiled=True)
+    me = lax.axis_index(axis)
+    parts = [x]
+    sources = [me]
+    for k in range(1, n):
+        parts.append(lax.ppermute(x, axis, line_pairs(n, k, True)))
+        sources.append(me - k)
+        parts.append(lax.ppermute(x, axis, line_pairs(n, k, False)))
+        sources.append(me + k)
+    out = jnp.zeros((n,) + x.shape, x.dtype)
+    for part, src in zip(parts, sources):
+        ok = (src >= 0) & (src < n)
+        out = lax.dynamic_update_index_in_dim(
+            out, jnp.where(ok, part, out[jnp.clip(src, 0, n - 1)]), jnp.clip(src, 0, n - 1), 0
+        )
+    return out.reshape((n * x.shape[0],) + x.shape[1:])
+
+
+def line_reduce_scatter(x, axis, wire):
+    n = lax.axis_size(axis)
+    if n > LINE_MAX:
+        return lax.psum_scatter(x, axis, scatter_dimension=0, tiled=True)
+    me = lax.axis_index(axis)
+    chunks = x.reshape((n, x.shape[0] // n) + x.shape[1:])
+    acc = lax.dynamic_index_in_dim(chunks, me, keepdims=False)
+    for k in range(1, n):
+        for rightward in (True, False):
+            dest = jnp.clip(me + k if rightward else me - k, 0, n - 1)
+            sent = lax.dynamic_index_in_dim(chunks, dest, keepdims=False).astype(wire)
+            got = lax.ppermute(sent, axis, line_pairs(n, k, rightward))
+            acc = acc + got.astype(x.dtype)
+    return acc
+
+
 def shards(acts, enc_weight, enc_bias, dec_weight, dec_bias, active_blocks, block_counts):
     local_enc = enc_weight[0]
     local_dec = dec_weight[:, 0, :]
     width, n_lat = local_enc.shape
-    tokens_all = lax.all_gather(acts, "latent", axis=1, tiled=True)[0]
+    tokens_all = line_gather(acts[0], "latent")
     n_tok = tokens_all.shape[0]
     tiles = n_tok // TILE
     blocks_local = n_lat // BLOCK
@@ -136,7 +180,7 @@
         count, flat_order, flat_blocks, codes, local_dec,
         2 * pairs * TILE * BLOCK * local_dec.shape[1], pairs * BLOCK * local_dec.shape[1] * 2,
     )
-    rebuilt = lax.psum_scatter(partial, "latent", scatter_dimension=0, tiled=True)
+    rebuilt = line_reduce_scatter(partial, "latent", jnp.bfloat16)
     return (rebuilt + dec_bias).astype(jnp.bfloat16)[None]
 
 

time: 191 us -> 189 us (0.990)
  waiting for transfers between devices: 143 us -> 101 us
  starting transfers between devices: 0.12 us -> 41.1 us
  Pallas kernels: 20.7 us -> 15.3 us
  local copies, waits for them, and re-layouts: 5.38 us -> 8.6 us
    reduce_scatter x1 -> x0, waiting for transfers between devices: 42.3 us -> none  [shards(): lax.psum_scatter(partial, 'latent', scatter_dimension=0, tiled=True)]
    ppermute x0 -> x12, starting transfers between devices: none -> 41 us  [the longest x6 20 us: line_reduce_scatter(): got = lax.ppermute(sent, axis, line_pairs(n, k, rightward))]
    all_gather x1 -> x0, waiting for transfers between devices: 24.3 us -> none  [shards(): tokens_all = lax.all_gather(acts, 'latent', axis=1, tiled=True)[0]]
    ppermute x0 -> x12, waiting for transfers between devices: none -> 23.8 us  [the longest x6 15.4 us: line_reduce_scatter(): got = lax.ppermute(sent, axis, line_pairs(n, k, rightward))]
    pallas_call x2, Pallas kernels: 20.7 us -> 15.3 us  [sparse_call(): pl.pallas_call(kernel, out_shape=out_shape, in_specs=[smem, smem, smem, p...]
    convert_element_type x0 -> x1, local copies, waits for them, and re-layouts: none -> 2.05 us  [line_reduce_scatter(): sent = lax.dynamic_index_in_dim(chunks, dest, keepdims=False).astype(wire)]
  transfers between devices with their start and end apart: 4 -> 14, of which waited for: 4 -> 5; matrix products, arithmetic and copies ran while one was open for 5% -> 5% of each run, Pallas kernels for 0% -> 0%
where the time goes in v4:
time: 189 us; the launch traced here: 188 us
  waiting for transfers between devices  101 us (53%)
  starting transfers between devices  41.1 us (22%)
  Pallas kernels  15.3 us (8%)
  between operations  13.7 us (7%)
  other arithmetic  8.63 us (5%)
  local copies, waits for them, and re-layouts  8.6 us (5%)
    reduce_scatter x1, waiting for transfers between devices, shards(): lax.psum_scatter(compact, ('section', 'tok'), scatter_dimension=2, tiled=...  48.4 us
    all_gather x1, waiting for transfers between devices, shards(): codes = lax.all_gather(codes_part, ('section', 'tok'), axis=2, tiled=True)  28.4 us
    ppermute x6, starting transfers between devices, line_reduce_scatter(): got = lax.ppermute(sent, axis, line_pairs(n, k, rightward))  20 us
    ppermute x3, starting transfers between devices, line_gather(): parts.append(lax.ppermute(x, axis, line_pairs(n, k, True)))  17.1 us
    ppermute x6, waiting for transfers between devices, line_reduce_scatter(): got = lax.ppermute(sent, axis, line_pairs(n, k, rightward))  15.4 us
    pallas_call x2, Pallas kernels, sparse_call(): pl.pallas_call(kernel, out_shape=out_shape, in_specs=[smem, smem, smem, p...  15.3 us
    ppermute x3, waiting for transfers between devices, line_gather(): parts.append(lax.ppermute(x, axis, line_pairs(n, k, False)))  8.44 us
    ppermute x3, starting transfers between devices, line_gather(): parts.append(lax.ppermute(x, axis, line_pairs(n, k, False)))  3.88 us
  transfers between devices with their start and end apart: 14, of which 5 were waited for; matrix products, arithmetic and copies ran while one was open for 5% of the time, Pallas kernels for 0%

profile of v4, /device:TPU:0, one launch (start us, length us, event | category | flops | bytes accessed | tf_op | source)
XLA Modules:
  0.0 187.9 jit_solution(14662505832718154030)
XLA Ops:
  6.5 5.1 %collective-permute-start = (bf16[64,2048]{1,0:T(8,128)(2,1)}, bf16[64,2048]{1,0:T(8,128)(2,1)S(1)}, u32[]{:S(2)}, u32[]{:S(2)}) collective-permute-start(bf16[64,2048]{1,0:T(8,128)(2,1)} %bitcast.89), channel_id=1, source_target_pairs={{0,4},{4,8},{8,12},{1,5},{5,9},{9,13},{2,6},{6,10},{10,14},{3,7},{... | collective-permute-start | bytes 786440 | tf_op jit(solution)/shard_map/ppermute | solution.py:116
  11.6 1.3 collective-permute-start.1
  12.9 5.6 %collective-permute-start.2 = (bf16[64,2048]{1,0:T(8,128)(2,1)}, bf16[64,2048]{1,0:T(8,128)(2,1)S(1)}, u32[]{:S(2)}, u32[]{:S(2)}) collective-permute-start(bf16[64,2048]{1,0:T(8,128)(2,1)} %bitcast.91), channel_id=1, source_target_pairs={{0,8},{4,12},{1,9},{5,13},{2,10},{6,14},{3,11},{7,15},{16,24},{20,... | collective-permute-start | bytes 786440 | tf_op jit(solution)/shard_map/ppermute | solution.py:116
  18.5 1.3 collective-permute-start.3
  19.8 6.5 %collective-permute-start.4 = (bf16[64,2048]{1,0:T(8,128)(2,1)}, bf16[64,2048]{1,0:T(8,128)(2,1)S(1)}, u32[]{:S(2)}, u32[]{:S(2)}) collective-permute-start(bf16[64,2048]{1,0:T(8,128)(2,1)} %bitcast.93), channel_id=1, source_target_pairs={{0,12},{1,13},{2,14},{3,15},{16,28},{17,29},{18,30},{19,31}} | collective-permute-start | bytes 786440 | tf_op jit(solution)/shard_map/ppermute | solution.py:116
  26.3 0.8 not_convert_fusion.1
  27.2 0.8 sort.34
  28.1 0.9 gather_fusion.2
  29.1 0.9 gather_fusion.3
  30.2 2.0 %sort.35 = (s32[64]{0:T(128)}, s32[64]{0:T(128)S(1)}) sort(s32[64]{0:T(128)S(1)} %reshape.94, s32[64]{0:T(128)S(1)} %iota.16), dimensions={0}, to_apply=%region_2.3 | sort | flops 384 | bytes 1024 | tf_op jit(solution)/shard_map/jit(argsort)/sort | solution.py:23
  32.4 0.6 convert_reduce_fusion
  33.1 1.3 gather_fusion
  34.4 1.3 collective-permute-start.5
  36.3 8.4 %collective-permute-done.5 = bf16[64,2048]{1,0:T(8,128)(2,1)S(1)} collective-permute-done((bf16[64,2048]{1,0:T(8,128)(2,1)S(1)}, bf16[64,2048]{1,0:T(8,128)(2,1)S(1)}, u32[]{:S(2)}, u32[]{:S(2)}) %collective-permute-start.5) | collective-permute-done | bytes 262176 | tf_op jit(solution)/shard_map/ppermute | solution.py:118
  44.8 1.0 copy-done.1
  45.8 7.8 %shard_map.73 = f32[2,32,128,128]{3,2,1,0:T(8,128)} custom-call(s32[1]{0:T(128)} %bitcast.1.n_ref, s32[64]{0:T(128)} %copy-done.4, s32[64]{0:T(128)} %gather_fusion, bf16[256,2048]{1,0:T(8,128)(2,1)} %bitcast.86, bf16[2048,8192]{1,0:T(8,128)(2,1)} %bitcast.84), custom_call_target="tpu_custom_call" | custom-call | flops 4294967296 | bytes 37748736 | tf_op jit(solution)/shard_map/pallas_call | solution.py:91
  53.7 0.9 scatter_custom_fusion
  54.8 0.6 gather_fusion.1
  55.4 48.4 %reduce-scatter.2.cloned.1.call-done = f32[2,32,16,128]{3,2,1,0:T(8,128)} async-done(((f32[2,32,128,128]{3,2,1,0:T(8,128)}), f32[2,32,16,128]{3,2,1,0:T(8,128)}) %reduce-scatter.2.cloned.1.call-update) | async-done | bytes 524304 | tf_op jit(solution)/shard_map/reduce_scatter | solution.py:167
  103.7 1.9 %select_convert_fusion = bf16[2,32,16,128]{3,2,1,0:T(8,128)(2,1)} fusion(f32[2,32,16,128]{3,2,1,0:T(8,128)} %reduce-scatter.2.cloned.1.call-done, f32[2,32,128]{2,1,0:T(8,128)S(1)} %bitcast.95, pred[2,32]{1,0:T(4,128)(4,1)S(1)} %get-tuple-element.10), kind=kLoop, calls=%fused_computation.19 | loop fusion | flops 524288 | bytes 819264 | tf_op jit(solution)/shard_map/convert_element_type | solution.py:173
  105.7 28.4 %all-gather.2.cloned.1.call-done.codes_ref = bf16[2,32,128,128]{3,2,1,0:T(8,128)(2,1)} async-done(((bf16[2,32,16,128]{3,2,1,0:T(8,128)(2,1)}), bf16[2,32,128,128]{3,2,1,0:T(8,128)(2,1)}) %all-gather.2.cloned.1.call-update) | async-done | bytes 2097168 | tf_op jit(solution)/shard_map/all_gather | solution.py:174
  134.0 7.5 %shard_map.74 = f32[256,2048]{1,0:T(8,128)} custom-call(s32[1]{0:T(128)} %bitcast.1.n_ref, s32[64]{0:T(128)} %copy-done.4, s32[64]{0:T(128)} %gather_fusion, bf16[2,32,128,128]{3,2,1,0:T(8,128)(2,1)} %all-gather.2.cloned.1.call-done.codes_ref, bf16[8192,2048]{1,0:T(8,128)(2,1)} %bitcast.85), custom_call_target="tpu_custom_call" | custom-call | flops 4294967296 | bytes 33554432 | tf_op jit(solution)/shard_map/pallas_call | solution.py:91
  141.5 2.0 %fusion.7 = (bf16[64,2048]{1,0:T(8,128)(2,1)S(1)}, bf16[64,2048]{1,0:T(8,128)(2,1)S(1)}, bf16[64,2048]{1,0:T(8,128)(2,1)S(1)}, bf16[64,2048]{1,0:T(8,128)(2,1)S(...) fusion(f32[4,64,2048]{2,1,0:T(8,128)} %bitcast.87, s32[]{:T(128)S(6)} %min.36, s32[]{:T(128)S(6)} %min.39, ...), kind=kLoop, calls=%fused_computation.20 | loop fusion | bytes 3145752 | tf_op jit(solution)/shard_map/convert_element_type | solution.py:139
  143.6 6.7 %collective-permute-start.10 = (bf16[64,2048]{1,0:T(8,128)(2,1)S(1)}, bf16[64,2048]{1,0:T(8,128)(2,1)S(1)}, u32[]{:S(2)}, u32[]{:S(2)}) collective-permute-start(bf16[64,2048]{1,0:T(8,128)(2,1)S(1)} %get-tuple-element.16), channel_id=1, source_target_pairs={{0,12},{1,13},{2,14},{3,15},{16,28},{17,29},{18,30},{19,31}} | collective-permute-start | bytes 786440 | tf_op jit(solution)/shard_map/ppermute | solution.py:140
  150.3 1.3 collective-permute-start.11
  151.6 1.3 collective-permute-start.6
  152.9 1.3 collective-permute-start.7
  154.2 8.2 %collective-permute-start.8 = (bf16[64,2048]{1,0:T(8,128)(2,1)S(1)}, bf16[64,2048]{1,0:T(8,128)(2,1)S(1)}, u32[]{:S(2)}, u32[]{:S(2)}) collective-permute-start(bf16[64,2048]{1,0:T(8,128)(2,1)S(1)} %get-tuple-element.18), channel_id=1, source_target_pairs={{0,8},{4,12},{1,9},{5,13},{2,10},{6,14},{3,11},{7,15},{16,24},{20,... | collective-permute-start | bytes 786440 | tf_op jit(solution)/shard_map/ppermute | solution.py:140
  162.4 1.3 collective-permute-start.9
  163.7 4.1 %collective-permute-done.7 = bf16[64,2048]{1,0:T(8,128)(2,1)S(1)} collective-permute-done((bf16[64,2048]{1,0:T(8,128)(2,1)S(1)}, bf16[64,2048]{1,0:T(8,128)(2,1)S(1)}, u32[]{:S(2)}, u32[]{:S(2)}) %collective-permute-start.7) | collective-permute-done | bytes 262176 | tf_op jit(solution)/shard_map/ppermute | solution.py:140
  167.8 11.2 %collective-permute-done.9 = bf16[64,2048]{1,0:T(8,128)(2,1)S(1)} collective-permute-done((bf16[64,2048]{1,0:T(8,128)(2,1)S(1)}, bf16[64,2048]{1,0:T(8,128)(2,1)S(1)}, u32[]{:S(2)}, u32[]{:S(2)}) %collective-permute-start.9) | collective-permute-done | bytes 262176 | tf_op jit(solution)/shard_map/ppermute | solution.py:140
  179.1 2.0 %fusion.13 = bf16[1,64,2048]{2,1,0:T(8,128)(2,1)} fusion(bf16[64,2048]{1,0:T(8,128)(2,1)S(1)} %collective-permute-done.11, bf16[64,2048]{1,0:T(8,128)(2,1)S(1)} %collective-permute-done.10, bf16[64,2048]{1,0:T(8,128)(2,1)S(1)} %collective-permute-done.9, bf16[64,2048]{1,0:T(8,128)(2,1)S(1)} %collective-permute-done.8, ...), kind=kLoop, calls=%fused_computation.26 | loop fusion | flops 1835008 | bytes 2367492 | tf_op jit(solution)/shard_map/broadcast_in_dim | solution.py:184
  (54 shorter events, 1.6 us)
Async XLA Ops:
  6.5 48.2 %copy-start = (f32[8192]{0:T(1024)S(1)}, f32[8192]{0:T(1024)}, u32[]{:S(2)}) copy-start(f32[8192]{0:T(1024)} %param.9) | copy-start | bytes 98308
  6.5 25.8 %copy-start.2 = (bf16[1,64,2048]{2,1,0:T(8,128)(2,1)S(1)}, bf16[1,64,2048]{2,1,0:T(8,128)(2,1)}, u32[]{:S(2)}) copy-start(bf16[1,64,2048]{2,1,0:T(8,128)(2,1)} %param.7) | copy-start | bytes 786436
  6.5 97.2 %reduce-scatter.2.cloned.1.call-start = ((), (), s32[]{:S(2)}) async-start(), calls=%async_computation.1 | async-start | bytes 4718592 | tf_op jit(solution)/shard_map/reduce_scatter | solution.py:167
  6.5 27.9 %collective-permute-start = (bf16[64,2048]{1,0:T(8,128)(2,1)}, bf16[64,2048]{1,0:T(8,128)(2,1)S(1)}, u32[]{:S(2)}, u32[]{:S(2)}) collective-permute-start(bf16[64,2048]{1,0:T(8,128)(2,1)} %bitcast.89), channel_id=1, source_target_pairs={{0,4},{4,8},{8,12},{1,5},{5,9},{9,13},{2,6},{6,10},{10,14},{3,7},{... | collective-permute-start | bytes 786440 | tf_op jit(solution)/shard_map/ppermute | solution.py:116
  11.6 24.2 %collective-permute-start.1 = (bf16[64,2048]{1,0:T(8,128)(2,1)}, bf16[64,2048]{1,0:T(8,128)(2,1)S(1)}, u32[]{:S(2)}, u32[]{:S(2)}) collective-permute-start(bf16[64,2048]{1,0:T(8,128)(2,1)} %bitcast.90), channel_id=1, source_target_pairs={{4,0},{8,4},{12,8},{5,1},{9,5},{13,9},{6,2},{10,6},{14,10},{7,3},{... | collective-permute-start | bytes 786440 | tf_op jit(solution)/shard_map/ppermute | solution.py:118
  12.9 23.1 %collective-permute-start.2 = (bf16[64,2048]{1,0:T(8,128)(2,1)}, bf16[64,2048]{1,0:T(8,128)(2,1)S(1)}, u32[]{:S(2)}, u32[]{:S(2)}) collective-permute-start(bf16[64,2048]{1,0:T(8,128)(2,1)} %bitcast.91), channel_id=1, source_target_pairs={{0,8},{4,12},{1,9},{5,13},{2,10},{6,14},{3,11},{7,15},{16,24},{20,... | collective-permute-start | bytes 786440 | tf_op jit(solution)/shard_map/ppermute | solution.py:116
  18.5 17.6 %collective-permute-start.3 = (bf16[64,2048]{1,0:T(8,128)(2,1)}, bf16[64,2048]{1,0:T(8,128)(2,1)S(1)}, u32[]{:S(2)}, u32[]{:S(2)}) collective-permute-start(bf16[64,2048]{1,0:T(8,128)(2,1)} %bitcast.92), channel_id=1, source_target_pairs={{8,0},{12,4},{9,1},{13,5},{10,2},{14,6},{11,3},{15,7},{24,16},{28,... | collective-permute-start | bytes 786440 | tf_op jit(solution)/shard_map/ppermute | solution.py:118
  19.8 16.4 %collective-permute-start.4 = (bf16[64,2048]{1,0:T(8,128)(2,1)}, bf16[64,2048]{1,0:T(8,128)(2,1)S(1)}, u32[]{:S(2)}, u32[]{:S(2)}) collective-permute-start(bf16[64,2048]{1,0:T(8,128)(2,1)} %bitcast.93), channel_id=1, source_target_pairs={{0,12},{1,13},{2,14},{3,15},{16,28},{17,29},{18,30},{19,31}} | collective-permute-start | bytes 786440 | tf_op jit(solution)/shard_map/ppermute | solution.py:116
  32.2 3.7 %copy-start.4 = (s32[64]{0:T(128)}, s32[64]{0:T(128)S(1)}, u32[]{:S(2)}) copy-start(s32[64]{0:T(128)S(1)} %get-tuple-element.8.slot_ref) | copy-start | bytes 772
  34.4 10.3 %collective-permute-start.5 = (bf16[64,2048]{1,0:T(8,128)(2,1)S(1)}, bf16[64,2048]{1,0:T(8,128)(2,1)S(1)}, u32[]{:S(2)}, u32[]{:S(2)}) collective-permute-start(bf16[64,2048]{1,0:T(8,128)(2,1)S(1)} %bitcast.94), channel_id=1, source_target_pairs={{12,0},{13,1},{14,2},{15,3},{28,16},{29,17},{30,18},{31,19}} | collective-permute-start | bytes 786440 | tf_op jit(solution)/shard_map/ppermute | solution.py:118
  44.8 1.0 copy-start.1
  53.6 80.4 %all-gather.2.cloned.1.call-start = ((), (), s32[]{:S(2)}) async-start(), calls=%async_computation.2 | async-start | bytes 2359296 | tf_op jit(solution)/shard_map/all_gather | solution.py:174
  141.5 37.6 %copy-start.3 = (f32[1,2048]{1,0:T(1,128)S(1)}, f32[1,2048]{1,0:T(1,128)}, u32[]{:S(2)}) copy-start(f32[1,2048]{1,0:T(1,128)} %param.11) | copy-start | bytes 24580
  143.6 18.8 %collective-permute-start.10 = (bf16[64,2048]{1,0:T(8,128)(2,1)S(1)}, bf16[64,2048]{1,0:T(8,128)(2,1)S(1)}, u32[]{:S(2)}, u32[]{:S(2)}) collective-permute-start(bf16[64,2048]{1,0:T(8,128)(2,1)S(1)} %get-tuple-element.16), channel_id=1, source_target_pairs={{0,12},{1,13},{2,14},{3,15},{16,28},{17,29},{18,30},{19,31}} | collective-permute-start | bytes 786440 | tf_op jit(solution)/shard_map/ppermute | solution.py:140
  150.3 13.4 %collective-permute-start.11 = (bf16[64,2048]{1,0:T(8,128)(2,1)S(1)}, bf16[64,2048]{1,0:T(8,128)(2,1)S(1)}, u32[]{:S(2)}, u32[]{:S(2)}) collective-permute-start(bf16[64,2048]{1,0:T(8,128)(2,1)S(1)} %get-tuple-element.15), channel_id=1, source_target_pairs={{12,0},{13,1},{14,2},{15,3},{28,16},{29,17},{30,18},{31,19}} | collective-permute-start | bytes 786440 | tf_op jit(solution)/shard_map/ppermute | solution.py:140
  151.6 12.1 %collective-permute-start.6 = (bf16[64,2048]{1,0:T(8,128)(2,1)S(1)}, bf16[64,2048]{1,0:T(8,128)(2,1)S(1)}, u32[]{:S(2)}, u32[]{:S(2)}) collective-permute-start(bf16[64,2048]{1,0:T(8,128)(2,1)S(1)} %get-tuple-element.14), channel_id=1, source_target_pairs={{0,4},{4,8},{8,12},{1,5},{5,9},{9,13},{2,6},{6,10},{10,14},{3,7},{... | collective-permute-start | bytes 786440 | tf_op jit(solution)/shard_map/ppermute | solution.py:140
  152.9 14.9 %collective-permute-start.7 = (bf16[64,2048]{1,0:T(8,128)(2,1)S(1)}, bf16[64,2048]{1,0:T(8,128)(2,1)S(1)}, u32[]{:S(2)}, u32[]{:S(2)}) collective-permute-start(bf16[64,2048]{1,0:T(8,128)(2,1)S(1)} %get-tuple-element.19), channel_id=1, source_target_pairs={{4,0},{8,4},{12,8},{5,1},{9,5},{13,9},{6,2},{10,6},{14,10},{7,3},{... | collective-permute-start | bytes 786440 | tf_op jit(solution)/shard_map/ppermute | solution.py:140
  154.2 13.6 %collective-permute-start.8 = (bf16[64,2048]{1,0:T(8,128)(2,1)S(1)}, bf16[64,2048]{1,0:T(8,128)(2,1)S(1)}, u32[]{:S(2)}, u32[]{:S(2)}) collective-permute-start(bf16[64,2048]{1,0:T(8,128)(2,1)S(1)} %get-tuple-element.18), channel_id=1, source_target_pairs={{0,8},{4,12},{1,9},{5,13},{2,10},{6,14},{3,11},{7,15},{16,24},{20,... | collective-permute-start | bytes 786440 | tf_op jit(solution)/shard_map/ppermute | solution.py:140
  162.4 16.7 %collective-permute-start.9 = (bf16[64,2048]{1,0:T(8,128)(2,1)S(1)}, bf16[64,2048]{1,0:T(8,128)(2,1)S(1)}, u32[]{:S(2)}, u32[]{:S(2)}) collective-permute-start(bf16[64,2048]{1,0:T(8,128)(2,1)S(1)} %get-tuple-element.17), channel_id=1, source_target_pairs={{8,0},{12,4},{9,1},{13,5},{10,2},{14,6},{11,3},{15,7},{24,16},{28,... | collective-permute-start | bytes 786440 | tf_op jit(solution)/shard_map/ppermute | solution.py:140
Sparse Core Ops, SparseCore 0:
  53.7 49.9 reduce-scatter.1
  105.8 28.1 all-gather.1

commit v5 on v4

--- a/solution.py
+++ b/solution.py
@@ -99,6 +99,7 @@
 
 
 LINE_MAX = 4
+FEW = 16
 
 
 def line_pairs(n, k, rightward):
@@ -150,36 +151,46 @@
     n_tok = tokens_all.shape[0]
     tiles = n_tok // TILE
     blocks_local = n_lat // BLOCK
-    slots = min(active_blocks.shape[1], blocks_local)
+    most = min(active_blocks.shape[1], blocks_local)
     first_block = lax.axis_index("latent") * blocks_local
-    picked_valid, count, flat_order, flat_blocks = slot_table(
-        active_blocks, block_counts, first_block, blocks_local, slots
-    )
-    pairs = tiles * slots
-
-    compact = sparse_call(
-        encode_kernel,
-        jax.ShapeDtypeStruct((tiles, slots, TILE, BLOCK), jnp.float32),
-        (width, BLOCK),
-        count, flat_order, flat_blocks, tokens_all, local_enc,
-        2 * pairs * TILE * width * BLOCK, pairs * (width * BLOCK * 2 + TILE * BLOCK * 4),
-    )
-    shared = lax.psum_scatter(compact, ("section", "tok"), scatter_dimension=2, tiled=True)
-    bias_slots = enc_bias.reshape(blocks_local, BLOCK)
-    slot_blocks = jnp.zeros((tiles * slots,), jnp.int32).at[flat_order].set(flat_blocks).reshape(tiles, slots)
-    bias_slots = bias_slots[slot_blocks]
-    codes_part = jnp.where(
-        picked_valid[:, :, None, None], jax.nn.relu(shared + bias_slots[:, :, None, :]), 0.0
-    ).astype(jnp.bfloat16)
-    codes = lax.all_gather(codes_part, ("section", "tok"), axis=2, tiled=True)
-
-    partial = sparse_call(
-        decode_kernel,
-        jax.ShapeDtypeStruct((n_tok, local_dec.shape[1]), jnp.float32),
-        (BLOCK, local_dec.shape[1]),
-        count, flat_order, flat_blocks, codes, local_dec,
-        2 * pairs * TILE * BLOCK * local_dec.shape[1], pairs * BLOCK * local_dec.shape[1] * 2,
-    )
+
+    def middle(slots):
+        picked_valid, count, flat_order, flat_blocks = slot_table(
+            active_blocks, block_counts, first_block, blocks_local, slots
+        )
+        pairs = tiles * slots
+        compact = sparse_call(
+            encode_kernel,
+            jax.ShapeDtypeStruct((tiles, slots, TILE, BLOCK), jnp.float32),
+            (width, BLOCK),
+            count, flat_order, flat_blocks, tokens_all, local_enc,
+            2 * pairs * TILE * width * BLOCK, pairs * (width * BLOCK * 2 + TILE * BLOCK * 4),
+        )
+        shared = lax.psum_scatter(compact, ("section", "tok"), scatter_dimension=2, tiled=True)
+        slot_blocks = jnp.zeros((pairs,), jnp.int32).at[flat_order].set(flat_blocks).reshape(tiles, slots)
+        bias_slots = enc_bias.reshape(blocks_local, BLOCK)[slot_blocks]
+        codes_part = jnp.where(
+            picked_valid[:, :, None, None], jax.nn.relu(shared + bias_slots[:, :, None, :]), 0.0
+        ).astype(jnp.bfloat16)
+        codes = lax.all_gather(codes_part, ("section", "tok"), axis=2, tiled=True)
+        return sparse_call(
+            decode_kernel,
+            jax.ShapeDtypeStruct((n_tok, local_dec.shape[1]), jnp.float32),
+            (BLOCK, local_dec.shape[1]),
+            count, flat_order, flat_blocks, codes, local_dec,
+            2 * pairs * TILE * BLOCK * local_dec.shape[1], pairs * BLOCK * local_dec.shape[1] * 2,
+        )
+
+    if most > FEW:
+        listed = jnp.arange(active_blocks.shape[1], dtype=jnp.int32)[None, :] < block_counts[:, None]
+        shard_of = active_blocks // blocks_local
+        per_shard = jnp.stack(
+            [jnp.sum((listed & (shard_of == s)).astype(jnp.int32), axis=1) for s in range(lax.axis_size("latent"))]
+        )
+        branch = (jnp.max(per_shard) > FEW).astype(jnp.int32)
+        partial = lax.switch(branch, [lambda: middle(FEW), lambda: middle(most)])
+    else:
+        partial = middle(most)
     rebuilt = line_reduce_scatter(partial, "latent", jnp.bfloat16)
     return (rebuilt + dec_bias).astype(jnp.bfloat16)[None]
 

time: 189 us -> 176 us (0.931)
  waiting for transfers between devices: 101 us -> 85.3 us
  other arithmetic: 8.63 us -> 12.1 us
  Pallas kernels: 15.3 us -> 12.4 us
  between operations: 13.7 us -> 16.2 us
  local copies, waits for them, and re-layouts: 8.6 us -> 6.19 us
    reduce_scatter x1, waiting for transfers between devices: 48.4 us -> 38 us  [middle(): lax.psum_scatter(compact, ('section', 'tok'), scatter_dimension=2, tiled=...]
    all_gather x1, waiting for transfers between devices: 28.4 us -> 23.9 us  [middle(): codes = lax.all_gather(codes_part, ('section', 'tok'), axis=2, tiled=True)]
    pallas_call x2, Pallas kernels: 15.3 us -> 12.4 us  [sparse_call(): pl.pallas_call(kernel, out_shape=out_shape, in_specs=[smem, smem, smem, p...]
    reduce_max x0 -> x4, other arithmetic: none -> 2.63 us  [shards(): branch = (jnp.max(per_shard) > FEW).astype(jnp.int32)]
  transfers between devices with their start and end apart: 14 -> 14, of which waited for: 5 -> 6; matrix products, arithmetic and copies ran while one was open for 5% -> 4% of each run, Pallas kernels for 0% -> 0%
where the time goes in v5:
time: 176 us; the launch traced here: 174 us
  waiting for transfers between devices  85.3 us (48%)
  starting transfers between devices  41.9 us (24%)
  between operations  16.2 us (9%)
  Pallas kernels  12.4 us (7%)
  other arithmetic  12.1 us (7%)
  local copies, waits for them, and re-layouts  6.19 us (4%)
    reduce_scatter x1, waiting for transfers between devices, middle(): lax.psum_scatter(compact, ('section', 'tok'), scatter_dimension=2, tiled=...  38 us
    all_gather x1, waiting for transfers between devices, middle(): codes = lax.all_gather(codes_part, ('section', 'tok'), axis=2, tiled=True)  23.9 us
    ppermute x6, starting transfers between devices, line_reduce_scatter(): got = lax.ppermute(sent, axis, line_pairs(n, k, rightward))  20.8 us
    ppermute x3, starting transfers between devices, line_gather(): parts.append(lax.ppermute(x, axis, line_pairs(n, k, True)))  17.1 us
    ppermute x6, waiting for transfers between devices, line_reduce_scatter(): got = lax.ppermute(sent, axis, line_pairs(n, k, rightward))  14.5 us
    pallas_call x2, Pallas kernels, sparse_call(): pl.pallas_call(kernel, out_shape=out_shape, in_specs=[smem, smem, smem, p...  12.4 us
    ppermute x3, waiting for transfers between devices, line_gather(): parts.append(lax.ppermute(x, axis, line_pairs(n, k, False)))  8.82 us
    ppermute x3, starting transfers between devices, line_gather(): parts.append(lax.ppermute(x, axis, line_pairs(n, k, False)))  3.88 us
  transfers between devices with their start and end apart: 14, of which 6 were waited for; matrix products, arithmetic and copies ran while one was open for 4% of the time, Pallas kernels for 0%

profile of v5, /device:TPU:0, one launch (start us, length us, event | category | flops | bytes accessed | tf_op | source)
XLA Modules:
  0.0 174.3 jit_solution(9973134009930677472)
XLA Ops:
  6.5 5.1 %collective-permute-start = (bf16[64,2048]{1,0:T(8,128)(2,1)}, bf16[64,2048]{1,0:T(8,128)(2,1)S(1)}, u32[]{:S(2)}, u32[]{:S(2)}) collective-permute-start(bf16[64,2048]{1,0:T(8,128)(2,1)} %bitcast.130), channel_id=1, source_target_pairs={{0,4},{4,8},{8,12},{1,5},{5,9},{9,13},{2,6},{6,10},{10,14},{3,7},{... | collective-permute-start | bytes 786440 | tf_op jit(solution)/shard_map/ppermute | solution.py:117
  11.6 1.3 collective-permute-start.1
  12.9 5.6 %collective-permute-start.2 = (bf16[64,2048]{1,0:T(8,128)(2,1)}, bf16[64,2048]{1,0:T(8,128)(2,1)S(1)}, u32[]{:S(2)}, u32[]{:S(2)}) collective-permute-start(bf16[64,2048]{1,0:T(8,128)(2,1)} %bitcast.132), channel_id=1, source_target_pairs={{0,8},{4,12},{1,9},{5,13},{2,10},{6,14},{3,11},{7,15},{16,24},{20,... | collective-permute-start | bytes 786440 | tf_op jit(solution)/shard_map/ppermute | solution.py:117
  18.5 1.3 collective-permute-start.3
  19.8 6.5 %collective-permute-start.4 = (bf16[64,2048]{1,0:T(8,128)(2,1)}, bf16[64,2048]{1,0:T(8,128)(2,1)S(1)}, u32[]{:S(2)}, u32[]{:S(2)}) collective-permute-start(bf16[64,2048]{1,0:T(8,128)(2,1)} %bitcast.134), channel_id=1, source_target_pairs={{0,12},{1,13},{2,14},{3,15},{16,28},{17,29},{18,30},{19,31}} | collective-permute-start | bytes 786440 | tf_op jit(solution)/shard_map/ppermute | solution.py:117
  26.5 1.0 select_dynamic-update-slice_fusion
  27.5 0.9 fusion.21
  29.0 0.7 reduce_max.24
  33.6 1.3 collective-permute-start.5
  35.2 8.8 %collective-permute-done.5 = bf16[64,2048]{1,0:T(8,128)(2,1)S(1)} collective-permute-done((bf16[64,2048]{1,0:T(8,128)(2,1)S(1)}, bf16[64,2048]{1,0:T(8,128)(2,1)S(1)}, u32[]{:S(2)}, u32[]{:S(2)}) %collective-permute-start.5) | collective-permute-done | bytes 262176 | tf_op jit(solution)/shard_map/ppermute | solution.py:119
  44.0 84.8 %conditional.1 = (f32[4,64,2048]{2,1,0:T(8,128)S(1)}) conditional(s32[]{:T(128)} %clamp.3, (s32[2]{0:T(128)S(1)}, s32[]{:T(128)}, s32[2,32]{1,0:T(2,128)S(1)}, s32[]{:T(128)}, bf16[4,64,2048]{2,1,0:T(8,128)(2,1)S(1)}, /*index=5*/s32[]{:T(128)}, bf16[64,2048]{1,0:T(8,128)(2,1)S(1)}, s32[]{:T(128)}, s32[]{:T(128)}, bf16[64,2048]{1,0:T(8,128)(2,1)S(1)}, ...), branch_computations={%region_8.14_spmd, %region_14.20_spmd} | conditional | flops 8590988288 | bytes 98688392 | solution.py:191
  44.2 0.8 sort.61
  45.2 0.7 gather_fusion.2
  46.0 0.8 gather_fusion.3
  47.6 1.6 sort.62
  49.7 1.3 gather_fusion
  51.1 6.6 %branch_0_fun.2 = f32[2,16,128,128]{3,2,1,0:T(8,128)} custom-call(s32[1]{0:T(128)} %bitcast.1.n_ref, s32[32]{0:T(128)} %copy-done.6, s32[32]{0:T(128)} %gather_fusion, bf16[256,2048]{1,0:T(8,128)(2,1)S(1)} %bitcast.124, bf16[2048,8192]{1,0:T(8,128)(2,1)} %bitcast.120), custom_call_target="tpu_custom_call" | custom-call | flops 2147483648 | bytes 18874368 | tf_op jit(solution)/shard_map/cond/branch_0_fun/pallas_call | solution.py:91
  57.8 0.8 scatter_custom_fusion
  59.4 38.0 %reduce-scatter.3.cloned.1.call-done = f32[2,16,16,128]{3,2,1,0:T(8,128)} async-done(((f32[2,16,128,128]{3,2,1,0:T(8,128)}), f32[2,16,16,128]{3,2,1,0:T(8,128)}) %reduce-scatter.3.cloned.1.call-update) | async-done | bytes 262160 | tf_op jit(solution)/shard_map/cond/branch_0_fun/reduce_scatter | solution.py:169
  97.3 1.7 select_convert_fusion
  99.1 23.9 %all-gather.3.cloned.1.call-done.codes_ref = bf16[2,16,128,128]{3,2,1,0:T(8,128)(2,1)} async-done(((bf16[2,16,16,128]{3,2,1,0:T(8,128)(2,1)}), bf16[2,16,128,128]{3,2,1,0:T(8,128)(2,1)}) %all-gather.3.cloned.1.call-update) | async-done | bytes 1048592 | tf_op jit(solution)/shard_map/cond/branch_0_fun/all_gather | solution.py:175
  123.0 5.8 %branch_0_fun.3 = f32[256,2048]{1,0:T(8,128)S(1)} custom-call(s32[1]{0:T(128)} %bitcast.1.n_ref, s32[32]{0:T(128)} %copy-done.6, s32[32]{0:T(128)} %gather_fusion, bf16[2,16,128,128]{3,2,1,0:T(8,128)(2,1)} %all-gather.3.cloned.1.call-done.codes_ref, bf16[8192,2048]{1,0:T(8,128)(2,1)} %bitcast.122), custom_call_target="tpu_custom_call" | custom-call | flops 2147483648 | bytes 16777216 | tf_op jit(solution)/shard_map/cond/branch_0_fun/pallas_call | solution.py:91
  129.0 6.1 %collective-permute-start.10 = (bf16[64,2048]{1,0:T(8,128)(2,1)S(1)}, bf16[64,2048]{1,0:T(8,128)(2,1)S(1)}, u32[]{:S(2)}, u32[]{:S(2)}) collective-permute-start(bf16[64,2048]{1,0:T(8,128)(2,1)S(1)} %get-tuple-element.281), channel_id=1, source_target_pairs={{0,12},{1,13},{2,14},{3,15},{16,28},{17,29},{18,30},{19,31}} | collective-permute-start | bytes 786440 | tf_op jit(solution)/shard_map/ppermute | solution.py:141
  135.2 1.3 collective-permute-start.11
  136.5 2.0 %collective-permute-start.6 = (bf16[64,2048]{1,0:T(8,128)(2,1)S(1)}, bf16[64,2048]{1,0:T(8,128)(2,1)}, u32[]{:S(2)}, u32[]{:S(2)}) collective-permute-start(bf16[64,2048]{1,0:T(8,128)(2,1)S(1)} %get-tuple-element.279), channel_id=1, source_target_pairs={{0,4},{4,8},{8,12},{1,5},{5,9},{9,13},{2,6},{6,10},{10,14},{3,7},{... | collective-permute-start | bytes 786440 | tf_op jit(solution)/shard_map/ppermute | solution.py:141
  138.5 1.3 collective-permute-start.7
  139.8 8.8 %collective-permute-start.8 = (bf16[64,2048]{1,0:T(8,128)(2,1)S(1)}, bf16[64,2048]{1,0:T(8,128)(2,1)}, u32[]{:S(2)}, u32[]{:S(2)}) collective-permute-start(bf16[64,2048]{1,0:T(8,128)(2,1)S(1)} %get-tuple-element.283), channel_id=1, source_target_pairs={{0,8},{4,12},{1,9},{5,13},{2,10},{6,14},{3,11},{7,15},{16,24},{20,... | collective-permute-start | bytes 786440 | tf_op jit(solution)/shard_map/ppermute | solution.py:141
  148.6 0.7 copy-done.2
  149.3 1.3 collective-permute-start.9
  150.6 2.1 %collective-permute-done.7 = bf16[64,2048]{1,0:T(8,128)(2,1)} collective-permute-done((bf16[64,2048]{1,0:T(8,128)(2,1)S(1)}, bf16[64,2048]{1,0:T(8,128)(2,1)}, u32[]{:S(2)}, u32[]{:S(2)}) %collective-permute-start.7) | collective-permute-done | bytes 262176 | tf_op jit(solution)/shard_map/ppermute | solution.py:141
  153.1 12.1 %collective-permute-done.9 = bf16[64,2048]{1,0:T(8,128)(2,1)} collective-permute-done((bf16[64,2048]{1,0:T(8,128)(2,1)S(1)}, bf16[64,2048]{1,0:T(8,128)(2,1)}, u32[]{:S(2)}, u32[]{:S(2)}) %collective-permute-start.9) | collective-permute-done | bytes 262176 | tf_op jit(solution)/shard_map/ppermute | solution.py:141
  165.2 2.3 %fusion.17 = bf16[1,64,2048]{2,1,0:T(8,128)(2,1)} fusion(bf16[64,2048]{1,0:T(8,128)(2,1)} %collective-permute-done.11, bf16[64,2048]{1,0:T(8,128)(2,1)} %copy-done.2, bf16[64,2048]{1,0:T(8,128)(2,1)} %collective-permute-done.9, bf16[64,2048]{1,0:T(8,128)(2,1)} %collective-permute-done.8, bf16[64,2048]{1,0:T(8,128)(2,1)} %collective-permute-done.7, ...), kind=kLoop, calls=%fused_computation.88 | loop fusion | flops 1835008 | bytes 2367492 | tf_op jit(solution)/shard_map/broadcast_in_dim | solution.py:195
  (64 shorter events, 5.4 us)
Async XLA Ops:
  6.5 27.1 %copy-start.1 = (bf16[1,64,2048]{2,1,0:T(8,128)(2,1)S(1)}, bf16[1,64,2048]{2,1,0:T(8,128)(2,1)}, u32[]{:S(2)}) copy-start(bf16[1,64,2048]{2,1,0:T(8,128)(2,1)} %param.9) | copy-start | bytes 786436
  6.5 27.1 %collective-permute-start = (bf16[64,2048]{1,0:T(8,128)(2,1)}, bf16[64,2048]{1,0:T(8,128)(2,1)S(1)}, u32[]{:S(2)}, u32[]{:S(2)}) collective-permute-start(bf16[64,2048]{1,0:T(8,128)(2,1)} %bitcast.130), channel_id=1, source_target_pairs={{0,4},{4,8},{8,12},{1,5},{5,9},{9,13},{2,6},{6,10},{10,14},{3,7},{... | collective-permute-start | bytes 786440 | tf_op jit(solution)/shard_map/ppermute | solution.py:117
  11.6 23.4 %collective-permute-start.1 = (bf16[64,2048]{1,0:T(8,128)(2,1)}, bf16[64,2048]{1,0:T(8,128)(2,1)S(1)}, u32[]{:S(2)}, u32[]{:S(2)}) collective-permute-start(bf16[64,2048]{1,0:T(8,128)(2,1)} %bitcast.131), channel_id=1, source_target_pairs={{4,0},{8,4},{12,8},{5,1},{9,5},{13,9},{6,2},{10,6},{14,10},{7,3},{... | collective-permute-start | bytes 786440 | tf_op jit(solution)/shard_map/ppermute | solution.py:119
  12.9 22.2 %collective-permute-start.2 = (bf16[64,2048]{1,0:T(8,128)(2,1)}, bf16[64,2048]{1,0:T(8,128)(2,1)S(1)}, u32[]{:S(2)}, u32[]{:S(2)}) collective-permute-start(bf16[64,2048]{1,0:T(8,128)(2,1)} %bitcast.132), channel_id=1, source_target_pairs={{0,8},{4,12},{1,9},{5,13},{2,10},{6,14},{3,11},{7,15},{16,24},{20,... | collective-permute-start | bytes 786440 | tf_op jit(solution)/shard_map/ppermute | solution.py:117
  18.5 16.7 %collective-permute-start.3 = (bf16[64,2048]{1,0:T(8,128)(2,1)}, bf16[64,2048]{1,0:T(8,128)(2,1)S(1)}, u32[]{:S(2)}, u32[]{:S(2)}) collective-permute-start(bf16[64,2048]{1,0:T(8,128)(2,1)} %bitcast.133), channel_id=1, source_target_pairs={{8,0},{12,4},{9,1},{13,5},{10,2},{14,6},{11,3},{15,7},{24,16},{28,... | collective-permute-start | bytes 786440 | tf_op jit(solution)/shard_map/ppermute | solution.py:119
  19.8 15.4 %collective-permute-start.4 = (bf16[64,2048]{1,0:T(8,128)(2,1)}, bf16[64,2048]{1,0:T(8,128)(2,1)S(1)}, u32[]{:S(2)}, u32[]{:S(2)}) collective-permute-start(bf16[64,2048]{1,0:T(8,128)(2,1)} %bitcast.134), channel_id=1, source_target_pairs={{0,12},{1,13},{2,14},{3,15},{16,28},{17,29},{18,30},{19,31}} | collective-permute-start | bytes 786440 | tf_op jit(solution)/shard_map/ppermute | solution.py:117
  26.3 17.7 %copy-start = (f32[8192]{0:T(1024)S(1)}, f32[8192]{0:T(1024)}, u32[]{:S(2)}) copy-start(f32[8192]{0:T(1024)} %param.11) | copy-start | bytes 98308
  26.3 17.7 %copy-start.3 = (s32[2,32]{1,0:T(2,128)S(1)}, s32[2,32]{1,0:T(2,128)}, u32[]{:S(2)}) copy-start(s32[2,32]{1,0:T(2,128)} %param.14) | copy-start | bytes 772
  26.3 17.7 %copy-start.5 = (s32[2]{0:T(128)S(1)}, s32[2]{0:T(128)}, u32[]{:S(2)}) copy-start(s32[2]{0:T(128)} %param.15) | copy-start | bytes 28
  33.6 10.3 %collective-permute-start.5 = (bf16[64,2048]{1,0:T(8,128)(2,1)S(1)}, bf16[64,2048]{1,0:T(8,128)(2,1)S(1)}, u32[]{:S(2)}, u32[]{:S(2)}) collective-permute-start(bf16[64,2048]{1,0:T(8,128)(2,1)S(1)} %bitcast.135), channel_id=1, source_target_pairs={{12,0},{13,1},{14,2},{15,3},{28,16},{29,17},{30,18},{31,19}} | collective-permute-start | bytes 786440 | tf_op jit(solution)/shard_map/ppermute | solution.py:119
  44.0 53.3 %reduce-scatter.3.cloned.1.call-start = ((), (), s32[]{:S(2)}) async-start(), calls=%async_computation.2 | async-start | bytes 2359296 | tf_op jit(solution)/shard_map/cond/branch_0_fun/reduce_scatter | solution.py:169
  49.2 0.5 copy-start.6
  57.7 65.2 %all-gather.3.cloned.1.call-start = ((), (), s32[]{:S(2)}) async-start(), calls=%async_computation.3 | async-start | bytes 1179648 | tf_op jit(solution)/shard_map/cond/branch_0_fun/all_gather | solution.py:175
  128.8 36.4 %copy-start.4 = (f32[1,2048]{1,0:T(1,128)S(1)}, f32[1,2048]{1,0:T(1,128)}, u32[]{:S(2)}) copy-start(f32[1,2048]{1,0:T(1,128)} %param.13) | copy-start | bytes 24580
  129.0 19.6 %collective-permute-start.10 = (bf16[64,2048]{1,0:T(8,128)(2,1)S(1)}, bf16[64,2048]{1,0:T(8,128)(2,1)S(1)}, u32[]{:S(2)}, u32[]{:S(2)}) collective-permute-start(bf16[64,2048]{1,0:T(8,128)(2,1)S(1)} %get-tuple-element.281), channel_id=1, source_target_pairs={{0,12},{1,13},{2,14},{3,15},{16,28},{17,29},{18,30},{19,31}} | collective-permute-start | bytes 786440 | tf_op jit(solution)/shard_map/ppermute | solution.py:141
  135.2 15.4 %collective-permute-start.11 = (bf16[64,2048]{1,0:T(8,128)(2,1)S(1)}, bf16[64,2048]{1,0:T(8,128)(2,1)}, u32[]{:S(2)}, u32[]{:S(2)}) collective-permute-start(bf16[64,2048]{1,0:T(8,128)(2,1)S(1)} %get-tuple-element.280), channel_id=1, source_target_pairs={{12,0},{13,1},{14,2},{15,3},{28,16},{29,17},{30,18},{31,19}} | collective-permute-start | bytes 786440 | tf_op jit(solution)/shard_map/ppermute | solution.py:141
  136.5 14.2 %collective-permute-start.6 = (bf16[64,2048]{1,0:T(8,128)(2,1)S(1)}, bf16[64,2048]{1,0:T(8,128)(2,1)}, u32[]{:S(2)}, u32[]{:S(2)}) collective-permute-start(bf16[64,2048]{1,0:T(8,128)(2,1)S(1)} %get-tuple-element.279), channel_id=1, source_target_pairs={{0,4},{4,8},{8,12},{1,5},{5,9},{9,13},{2,6},{6,10},{10,14},{3,7},{... | collective-permute-start | bytes 786440 | tf_op jit(solution)/shard_map/ppermute | solution.py:141
  138.5 14.3 %collective-permute-start.7 = (bf16[64,2048]{1,0:T(8,128)(2,1)S(1)}, bf16[64,2048]{1,0:T(8,128)(2,1)}, u32[]{:S(2)}, u32[]{:S(2)}) collective-permute-start(bf16[64,2048]{1,0:T(8,128)(2,1)S(1)} %get-tuple-element.284), channel_id=1, source_target_pairs={{4,0},{8,4},{12,8},{5,1},{9,5},{13,9},{6,2},{10,6},{14,10},{7,3},{... | collective-permute-start | bytes 786440 | tf_op jit(solution)/shard_map/ppermute | solution.py:141
  139.8 13.3 %collective-permute-start.8 = (bf16[64,2048]{1,0:T(8,128)(2,1)S(1)}, bf16[64,2048]{1,0:T(8,128)(2,1)}, u32[]{:S(2)}, u32[]{:S(2)}) collective-permute-start(bf16[64,2048]{1,0:T(8,128)(2,1)S(1)} %get-tuple-element.283), channel_id=1, source_target_pairs={{0,8},{4,12},{1,9},{5,13},{2,10},{6,14},{3,11},{7,15},{16,24},{20,... | collective-permute-start | bytes 786440 | tf_op jit(solution)/shard_map/ppermute | solution.py:141
  148.6 0.7 copy-start.2
  149.3 15.8 %collective-permute-start.9 = (bf16[64,2048]{1,0:T(8,128)(2,1)S(1)}, bf16[64,2048]{1,0:T(8,128)(2,1)}, u32[]{:S(2)}, u32[]{:S(2)}) collective-permute-start(bf16[64,2048]{1,0:T(8,128)(2,1)S(1)} %get-tuple-element.282), channel_id=1, source_target_pairs={{8,0},{12,4},{9,1},{13,5},{10,2},{14,6},{11,3},{15,7},{24,16},{28,... | collective-permute-start | bytes 786440 | tf_op jit(solution)/shard_map/ppermute | solution.py:141
Sparse Core Ops, SparseCore 0:
  57.9 39.4 reduce-scatter.2
  99.4 23.5 all-gather.2

commit v6 on v5

--- a/solution.py
+++ b/solution.py
@@ -143,11 +143,41 @@
     return acc
 
 
+def halving_steps():
+    steps = []
+    for axis in ("section", "tok"):
+        n = lax.axis_size(axis)
+        if n & (n - 1):
+            return None
+        me = lax.axis_index(axis)
+        level = n // 2
+        while level:
+            steps.append((axis, (me // level) % 2, [(i, i ^ level) for i in range(n)]))
+            level //= 2
+    return steps
+
+
+def halving_sum(x, steps):
+    for axis, bit, perm in steps:
+        half = x.shape[2] // 2
+        keep = lax.dynamic_slice_in_dim(x, bit * half, half, axis=2)
+        send = lax.dynamic_slice_in_dim(x, (1 - bit) * half, half, axis=2)
+        x = keep + lax.ppermute(send, axis, perm)
+    return x
+
+
+def doubling_gather(x, steps):
+    for axis, bit, perm in reversed(steps):
+        got = lax.ppermute(x, axis, perm)
+        x = jnp.where(bit == 0, jnp.concatenate([x, got], axis=2), jnp.concatenate([got, x], axis=2))
+    return x
+
+
 def shards(acts, enc_weight, enc_bias, dec_weight, dec_bias, active_blocks, block_counts):
     local_enc = enc_weight[0]
     local_dec = dec_weight[:, 0, :]
     width, n_lat = local_enc.shape
-    tokens_all = line_gather(acts[0], "latent")
+    tokens_all = lax.all_gather(acts, "latent", axis=1, tiled=True)[0]
     n_tok = tokens_all.shape[0]
     tiles = n_tok // TILE
     blocks_local = n_lat // BLOCK
@@ -166,13 +196,20 @@
             count, flat_order, flat_blocks, tokens_all, local_enc,
             2 * pairs * TILE * width * BLOCK, pairs * (width * BLOCK * 2 + TILE * BLOCK * 4),
         )
-        shared = lax.psum_scatter(compact, ("section", "tok"), scatter_dimension=2, tiled=True)
+        steps = halving_steps()
+        if steps is None:
+            shared = lax.psum_scatter(compact, ("section", "tok"), scatter_dimension=2, tiled=True)
+        else:
+            shared = halving_sum(compact, steps)
         slot_blocks = jnp.zeros((pairs,), jnp.int32).at[flat_order].set(flat_blocks).reshape(tiles, slots)
         bias_slots = enc_bias.reshape(blocks_local, BLOCK)[slot_blocks]
         codes_part = jnp.where(
             picked_valid[:, :, None, None], jax.nn.relu(shared + bias_slots[:, :, None, :]), 0.0
         ).astype(jnp.bfloat16)
-        codes = lax.all_gather(codes_part, ("section", "tok"), axis=2, tiled=True)
+        if steps is None:
+            codes = lax.all_gather(codes_part, ("section", "tok"), axis=2, tiled=True)
+        else:
+            codes = doubling_gather(codes_part, steps)
         return sparse_call(
             decode_kernel,
             jax.ShapeDtypeStruct((n_tok, local_dec.shape[1]), jnp.float32),

time: 176 us -> 146 us (0.83)
  waiting for transfers between devices: 85.3 us -> 68.2 us
  starting transfers between devices: 41.9 us -> 26.8 us
  Pallas kernels: 12.4 us -> 14.3 us
    reduce_scatter x1 -> x0, waiting for transfers between devices: 38 us -> none  [middle(): lax.psum_scatter(compact, ('section', 'tok'), scatter_dimension=2, tiled=...]
    ppermute x6, waiting for transfers between devices: 8.82 us -> 30 us  [the longest x3 19.7 us: halving_sum(): x = keep + lax.ppermute(send, axis, perm)]
    ppermute x6, starting transfers between devices: 21 us -> 6.3 us  [the longest x3 3.15 us: doubling_gather(): got = lax.ppermute(x, axis, perm)]
    ppermute x6, waiting for transfers between devices: 14.5 us -> 11.2 us  [line_reduce_scatter(): got = lax.ppermute(sent, axis, line_pairs(n, k, rightward))]
    all_gather x1, waiting for transfers between devices: 23.9 us -> 26.2 us  [shards(): tokens_all = lax.all_gather(acts, 'latent', axis=1, tiled=True)[0]]
    pallas_call x2, Pallas kernels: 12.4 us -> 14.3 us  [sparse_call(): pl.pallas_call(kernel, out_shape=out_shape, in_specs=[smem, smem, smem, p...]
  transfers between devices with their start and end apart: 14 -> 13, of which waited for: 6 -> 8; matrix products, arithmetic and copies ran while one was open for 4% -> 3% of each run, Pallas kernels for 0% -> 0%
where the time goes in v6:
time: 146 us
  waiting for transfers between devices  68.2 us (47%)
  starting transfers between devices  26.8 us (18%)
  between operations  16 us (11%)
  Pallas kernels  14.3 us (10%)
  other arithmetic  13.1 us (9%)
  local copies, waits for them, and re-layouts  7.32 us (5%)
    all_gather x1, waiting for transfers between devices, shards(): tokens_all = lax.all_gather(acts, 'latent', axis=1, tiled=True)[0]  26.2 us
    ppermute x6, starting transfers between devices, line_reduce_scatter(): got = lax.ppermute(sent, axis, line_pairs(n, k, rightward))  20.5 us
    ppermute x3, waiting for transfers between devices, halving_sum(): x = keep + lax.ppermute(send, axis, perm)  19.7 us
    pallas_call x2, Pallas kernels, sparse_call(): pl.pallas_call(kernel, out_shape=out_shape, in_specs=[smem, smem, smem, p...  14.3 us
    ppermute x6, waiting for transfers between devices, line_reduce_scatter(): got = lax.ppermute(sent, axis, line_pairs(n, k, rightward))  11.2 us
    ppermute x3, waiting for transfers between devices, doubling_gather(): got = lax.ppermute(x, axis, perm)  10.3 us
    ppermute x3, starting transfers between devices, doubling_gather(): got = lax.ppermute(x, axis, perm)  3.15 us
    ppermute x3, starting transfers between devices, halving_sum(): x = keep + lax.ppermute(send, axis, perm)  3.14 us
  transfers between devices with their start and end apart: 13, of which 8 were waited for; matrix products, arithmetic and copies ran while one was open for 3% of the time, Pallas kernels for 0%

profile of v6, /device:TPU:0, one launch (start us, length us, event | category | flops | bytes accessed | tf_op | source)
XLA Modules:
  0.0 145.9 jit_solution(6070104880286581241)
XLA Ops:
  7.3 0.9 fusion.21
  13.4 26.2 %all-gather.2.cloned.1.call-done = bf16[1,256,2048]{2,1,0:T(8,128)(2,1)} async-done(((bf16[1,64,2048]{2,1,0:T(8,128)(2,1)}), bf16[1,256,2048]{2,1,0:T(8,128)(2,1)}) %all-gather.2.cloned.1.call-update) | async-done | bytes 1048592 | tf_op jit(solution)/shard_map/all_gather | solution.py:180
  39.6 64.4 %conditional.1 = (f32[4,64,2048]{2,1,0:T(8,128)S(1)}) conditional(s32[]{:T(128)} %clamp.3, (s32[2]{0:T(128)}, s32[]{:T(128)}, s32[2,32]{1,0:T(2,128)}, bf16[1,256,2048]{2,1,0:T(8,128)(2,1)}, bf16[1,2048,8192]{2,1,0:T(8,128)(2,1)}, /*index=5*/f32[8192]{0:T(1024)}, bf16[8192,1,2048]{2,0,1:T(8,128)(2,1)}) %tuple.14, (s32[2]{0:T(128)}, s32[]{:T(128)}, ...), branch_computations={%region_8.13_spmd, %region_13.18_spmd} | conditional | flops 8607896576 | bytes 123199736 | solution.py:228
  39.6 0.9 not_convert_fusion.1
  40.5 0.8 sort.61
  42.4 0.8 gather_fusion.3
  43.9 1.7 %sort.62 = (s32[32]{0:T(128)}, s32[32]{0:T(128)S(1)}) sort(s32[32]{0:T(128)S(1)} %reshape.170, s32[32]{0:T(128)S(1)} %iota.29), dimensions={0}, to_apply=%region_11.11 | sort | flops 160 | bytes 512 | tf_op jit(solution)/shard_map/cond/branch_0_fun/jit(argsort)/sort | solution.py:23
  45.7 1.2 gather_fusion
  46.9 7.6 %branch_0_fun.2 = f32[2,16,128,128]{3,2,1,0:T(8,128)} custom-call(s32[1]{0:T(128)} %bitcast.1.n_ref, s32[32]{0:T(128)} %copy-done.7, s32[32]{0:T(128)} %gather_fusion, bf16[256,2048]{1,0:T(8,128)(2,1)S(1)} %bitcast.67, bf16[2048,8192]{1,0:T(8,128)(2,1)} %bitcast.59), custom_call_target="tpu_custom_call" | custom-call | flops 2147483648 | bytes 18874368 | tf_op jit(solution)/shard_map/cond/branch_0_fun/pallas_call | solution.py:91
  54.5 1.5 constant_dynamic-slice_fusion.2
  56.1 2.7 %collective-permute-done = f32[2,16,64,128]{3,2,1,0:T(8,128)} collective-permute-done((f32[2,16,64,128]{3,2,1,0:T(8,128)S(1)}, f32[2,16,64,128]{3,2,1,0:T(8,128)}, u32[]{:S(2)}, u32[]{:S(2)}) %collective-permute-start) | collective-permute-done | bytes 1048608 | tf_op jit(solution)/shard_map/cond/branch_0_fun/ppermute | solution.py:165
  58.9 1.4 dynamic-slice_add_fusion
  60.3 1.5 %collective-permute-start.1 = (f32[2,16,32,128]{3,2,1,0:T(8,128)S(1)}, f32[2,16,32,128]{3,2,1,0:T(8,128)S(1)}, u32[]{:S(2)}, u32[]{:S(2)}) collective-permute-start(f32[2,16,32,128]{3,2,1,0:T(8,128)S(1)} %constant_dynamic-slice_fusion.1), channel_id=1, source_target_pairs={{0,2},{1,3},{2,0},{3,1},{4,6},{5,7},{6,4},{7,5},{8,10},{9,11},{10,... | collective-permute-start | bytes 1572872 | tf_op jit(solution)/shard_map/cond/branch_0_fun/ppermute | solution.py:165
  61.8 0.8 scatter_custom_fusion
  62.7 11.6 %collective-permute-done.1 = f32[2,16,32,128]{3,2,1,0:T(8,128)S(1)} collective-permute-done((f32[2,16,32,128]{3,2,1,0:T(8,128)S(1)}, f32[2,16,32,128]{3,2,1,0:T(8,128)S(1)}, u32[]{:S(2)}, u32[]{:S(2)}) %collective-permute-start.1) | collective-permute-done | bytes 524320 | tf_op jit(solution)/shard_map/cond/branch_0_fun/ppermute | solution.py:165
  74.4 1.5 %collective-permute-start.2 = (f32[2,16,16,128]{3,2,1,0:T(8,128)S(1)}, f32[2,16,16,128]{3,2,1,0:T(8,128)S(1)}, u32[]{:S(2)}, u32[]{:S(2)}) collective-permute-start(f32[2,16,16,128]{3,2,1,0:T(8,128)S(1)} %constant_dynamic-slice_fusion), channel_id=1, source_target_pairs={{0,1},{1,0},{2,3},{3,2},{4,5},{5,4},{6,7},{7,6},{8,9},{9,8},{10,11... | collective-permute-start | bytes 786440 | tf_op jit(solution)/shard_map/cond/branch_0_fun/ppermute | solution.py:165
  76.6 5.4 %collective-permute-done.2 = f32[2,16,16,128]{3,2,1,0:T(8,128)S(1)} collective-permute-done((f32[2,16,16,128]{3,2,1,0:T(8,128)S(1)}, f32[2,16,16,128]{3,2,1,0:T(8,128)S(1)}, u32[]{:S(2)}, u32[]{:S(2)}) %collective-permute-start.2) | collective-permute-done | bytes 262176 | tf_op jit(solution)/shard_map/cond/branch_0_fun/ppermute | solution.py:165
  82.1 1.5 %collective-permute-start.3 = (bf16[2,16,16,128]{3,2,1,0:T(8,128)(2,1)S(1)}, bf16[2,16,16,128]{3,2,1,0:T(8,128)(2,1)S(1)}, u32[]{:S(2)}, u32[]{:S(2)}) collective-permute-start(bf16[2,16,16,128]{3,2,1,0:T(8,128)(2,1)S(1)} %select_convert_fusion), channel_id=1, source_target_pairs={{0,1},{1,0},{2,3},{3,2},{4,5},{5,4},{6,7},{7,6},{8,9},{9,8},{10,11... | collective-permute-start | bytes 393224 | tf_op jit(solution)/shard_map/cond/branch_0_fun/ppermute | solution.py:171
  83.7 3.5 %collective-permute-done.3 = bf16[2,16,16,128]{3,2,1,0:T(8,128)(2,1)S(1)} collective-permute-done((bf16[2,16,16,128]{3,2,1,0:T(8,128)(2,1)S(1)}, bf16[2,16,16,128]{3,2,1,0:T(8,128)(2,1)S(1)}, u32[]{:S(2)}, u32[]{:S(2)}) %collective-permute-start.3) | collective-permute-done | bytes 131104 | tf_op jit(solution)/shard_map/cond/branch_0_fun/ppermute | solution.py:171
  87.3 1.5 %collective-permute-start.4 = (bf16[2,16,32,128]{3,2,1,0:T(8,128)(2,1)S(1)}, bf16[2,16,32,128]{3,2,1,0:T(8,128)(2,1)S(1)}, u32[]{:S(2)}, u32[]{:S(2)}) collective-permute-start(bf16[2,16,32,128]{3,2,1,0:T(8,128)(2,1)S(1)} %maximum_select_fusion.2), channel_id=1, source_target_pairs={{0,2},{1,3},{2,0},{3,1},{4,6},{5,7},{6,4},{7,5},{8,10},{9,11},{10,... | collective-permute-start | bytes 786440 | tf_op jit(solution)/shard_map/cond/branch_0_fun/ppermute | solution.py:171
  88.8 4.9 %collective-permute-done.4 = bf16[2,16,32,128]{3,2,1,0:T(8,128)(2,1)S(1)} collective-permute-done((bf16[2,16,32,128]{3,2,1,0:T(8,128)(2,1)S(1)}, bf16[2,16,32,128]{3,2,1,0:T(8,128)(2,1)S(1)}, u32[]{:S(2)}, u32[]{:S(2)}) %collective-permute-start.4) | collective-permute-done | bytes 262176 | tf_op jit(solution)/shard_map/cond/branch_0_fun/ppermute | solution.py:171
  94.0 1.9 %collective-permute-done.5 = bf16[2,16,64,128]{3,2,1,0:T(8,128)(2,1)S(1)} collective-permute-done((bf16[2,16,64,128]{3,2,1,0:T(8,128)(2,1)S(1)}, bf16[2,16,64,128]{3,2,1,0:T(8,128)(2,1)S(1)}, u32[]{:S(2)}, u32[]{:S(2)}) %collective-permute-start.5) | collective-permute-done | bytes 524320 | tf_op jit(solution)/shard_map/cond/branch_0_fun/ppermute | solution.py:171
  95.9 1.4 maximum_select_fusion.codes_ref
  97.2 6.8 %branch_0_fun.3 = f32[256,2048]{1,0:T(8,128)S(1)} custom-call(s32[1]{0:T(128)} %bitcast.1.n_ref, s32[32]{0:T(128)} %copy-done.7, s32[32]{0:T(128)} %gather_fusion, bf16[2,16,128,128]{3,2,1,0:T(8,128)(2,1)} %maximum_select_fusion.codes_ref, bf16[8192,2048]{1,0:T(8,128)(2,1)} %bitcast.61), custom_call_target="tpu_custom_call" | custom-call | flops 2147483648 | bytes 16777216 | tf_op jit(solution)/shard_map/cond/branch_0_fun/pallas_call | solution.py:91
  104.3 4.5 %collective-permute-start.12 = (bf16[64,2048]{1,0:T(8,128)(2,1)S(1)}, bf16[64,2048]{1,0:T(8,128)(2,1)S(1)}, u32[]{:S(2)}, u32[]{:S(2)}) collective-permute-start(bf16[64,2048]{1,0:T(8,128)(2,1)S(1)} %get-tuple-element.79), channel_id=1, source_target_pairs={{0,4},{4,8},{8,12},{1,5},{5,9},{9,13},{2,6},{6,10},{10,14},{3,7},{... | collective-permute-start | bytes 786440 | tf_op jit(solution)/shard_map/ppermute | solution.py:141
  108.8 1.3 collective-permute-start.13
  110.1 4.7 %collective-permute-start.14 = (bf16[64,2048]{1,0:T(8,128)(2,1)S(1)}, bf16[64,2048]{1,0:T(8,128)(2,1)}, u32[]{:S(2)}, u32[]{:S(2)}) collective-permute-start(bf16[64,2048]{1,0:T(8,128)(2,1)S(1)} %get-tuple-element.83), channel_id=1, source_target_pairs={{0,8},{4,12},{1,9},{5,13},{2,10},{6,14},{3,11},{7,15},{16,24},{20,... | collective-permute-start | bytes 786440 | tf_op jit(solution)/shard_map/ppermute | solution.py:141
  114.8 1.3 collective-permute-start.15
  116.1 7.4 %collective-permute-start.16 = (bf16[64,2048]{1,0:T(8,128)(2,1)S(1)}, bf16[64,2048]{1,0:T(8,128)(2,1)}, u32[]{:S(2)}, u32[]{:S(2)}) collective-permute-start(bf16[64,2048]{1,0:T(8,128)(2,1)S(1)} %get-tuple-element.81), channel_id=1, source_target_pairs={{0,12},{1,13},{2,14},{3,15},{16,28},{17,29},{18,30},{19,31}} | collective-permute-start | bytes 786440 | tf_op jit(solution)/shard_map/ppermute | solution.py:141
  124.2 1.3 collective-permute-start.17
  125.5 11.2 %collective-permute-done.15 = bf16[64,2048]{1,0:T(8,128)(2,1)} collective-permute-done((bf16[64,2048]{1,0:T(8,128)(2,1)S(1)}, bf16[64,2048]{1,0:T(8,128)(2,1)}, u32[]{:S(2)}, u32[]{:S(2)}) %collective-permute-start.15) | collective-permute-done | bytes 262176 | tf_op jit(solution)/shard_map/ppermute | solution.py:141
  136.7 2.3 %fusion.17 = bf16[1,64,2048]{2,1,0:T(8,128)(2,1)} fusion(bf16[64,2048]{1,0:T(8,128)(2,1)} %collective-permute-done.17, bf16[64,2048]{1,0:T(8,128)(2,1)} %collective-permute-done.16, bf16[64,2048]{1,0:T(8,128)(2,1)} %collective-permute-done.15, bf16[64,2048]{1,0:T(8,128)(2,1)} %collective-permute-done.14, bf16[64,2048]{1,0:T(8,128)(2,1)} %collective-permute-done.13, ...), kind=kLoop, calls=%fused_computation.80 | loop fusion | flops 1835008 | bytes 2367492 | tf_op jit(solution)/shard_map/broadcast_in_dim | solution.py:232
  (53 shorter events, 7.7 us)
Async XLA Ops:
  6.5 33.1 %all-gather.2.cloned.1.call-start = ((), (), s32[]{:S(2)}) async-start(), calls=%async_computation | async-start | bytes 1310720 | tf_op jit(solution)/shard_map/all_gather | solution.py:180
  39.6 7.3 %copy-start.3 = (bf16[1,256,2048]{2,1,0:T(8,128)(2,1)S(1)}, bf16[1,256,2048]{2,1,0:T(8,128)(2,1)}, u32[]{:S(2)}) copy-start(bf16[1,256,2048]{2,1,0:T(8,128)(2,1)} %get-tuple-element.52) | copy-start | bytes 3145732 | tf_op jit(solution)/shard_map/cond
  45.6 1.3 copy-start.7
  54.5 4.3 %copy-start = (f32[2,16,128,128]{3,2,1,0:T(8,128)S(1)}, f32[2,16,128,128]{3,2,1,0:T(8,128)}, u32[]{:S(2)}) copy-start(f32[2,16,128,128]{3,2,1,0:T(8,128)} %branch_0_fun.2) | copy-start | bytes 6291460 | tf_op jit(solution)/shard_map/cond
  56.0 2.9 %collective-permute-start = (f32[2,16,64,128]{3,2,1,0:T(8,128)S(1)}, f32[2,16,64,128]{3,2,1,0:T(8,128)}, u32[]{:S(2)}, u32[]{:S(2)}) collective-permute-start(f32[2,16,64,128]{3,2,1,0:T(8,128)S(1)} %constant_dynamic-slice_fusion.2), channel_id=1, source_target_pairs={{0,16},{16,0},{1,17},{17,1},{2,18},{18,2},{3,19},{19,3},{4,20},{20... | collective-permute-start | bytes 3145736 | tf_op jit(solution)/shard_map/cond/branch_0_fun/ppermute | solution.py:165
  60.2 15.9 %copy-start.1 = (f32[8192]{0:T(1024)S(1)}, f32[8192]{0:T(1024)}, u32[]{:S(2)}) copy-start(f32[8192]{0:T(1024)} %get-tuple-element.54) | copy-start | bytes 98308 | tf_op jit(solution)/shard_map/cond
  60.3 14.0 %collective-permute-start.1 = (f32[2,16,32,128]{3,2,1,0:T(8,128)S(1)}, f32[2,16,32,128]{3,2,1,0:T(8,128)S(1)}, u32[]{:S(2)}, u32[]{:S(2)}) collective-permute-start(f32[2,16,32,128]{3,2,1,0:T(8,128)S(1)} %constant_dynamic-slice_fusion.1), channel_id=1, source_target_pairs={{0,2},{1,3},{2,0},{3,1},{4,6},{5,7},{6,4},{7,5},{8,10},{9,11},{10,... | collective-permute-start | bytes 1572872 | tf_op jit(solution)/shard_map/cond/branch_0_fun/ppermute | solution.py:165
  74.4 7.6 %collective-permute-start.2 = (f32[2,16,16,128]{3,2,1,0:T(8,128)S(1)}, f32[2,16,16,128]{3,2,1,0:T(8,128)S(1)}, u32[]{:S(2)}, u32[]{:S(2)}) collective-permute-start(f32[2,16,16,128]{3,2,1,0:T(8,128)S(1)} %constant_dynamic-slice_fusion), channel_id=1, source_target_pairs={{0,1},{1,0},{2,3},{3,2},{4,5},{5,4},{6,7},{7,6},{8,9},{9,8},{10,11... | collective-permute-start | bytes 786440 | tf_op jit(solution)/shard_map/cond/branch_0_fun/ppermute | solution.py:165
  82.1 5.0 %collective-permute-start.3 = (bf16[2,16,16,128]{3,2,1,0:T(8,128)(2,1)S(1)}, bf16[2,16,16,128]{3,2,1,0:T(8,128)(2,1)S(1)}, u32[]{:S(2)}, u32[]{:S(2)}) collective-permute-start(bf16[2,16,16,128]{3,2,1,0:T(8,128)(2,1)S(1)} %select_convert_fusion), channel_id=1, source_target_pairs={{0,1},{1,0},{2,3},{3,2},{4,5},{5,4},{6,7},{7,6},{8,9},{9,8},{10,11... | collective-permute-start | bytes 393224 | tf_op jit(solution)/shard_map/cond/branch_0_fun/ppermute | solution.py:171
  87.3 6.4 %collective-permute-start.4 = (bf16[2,16,32,128]{3,2,1,0:T(8,128)(2,1)S(1)}, bf16[2,16,32,128]{3,2,1,0:T(8,128)(2,1)S(1)}, u32[]{:S(2)}, u32[]{:S(2)}) collective-permute-start(bf16[2,16,32,128]{3,2,1,0:T(8,128)(2,1)S(1)} %maximum_select_fusion.2), channel_id=1, source_target_pairs={{0,2},{1,3},{2,0},{3,1},{4,6},{5,7},{6,4},{7,5},{8,10},{9,11},{10,... | collective-permute-start | bytes 786440 | tf_op jit(solution)/shard_map/cond/branch_0_fun/ppermute | solution.py:171
  93.9 2.0 %collective-permute-start.5 = (bf16[2,16,64,128]{3,2,1,0:T(8,128)(2,1)S(1)}, bf16[2,16,64,128]{3,2,1,0:T(8,128)(2,1)S(1)}, u32[]{:S(2)}, u32[]{:S(2)}) collective-permute-start(bf16[2,16,64,128]{3,2,1,0:T(8,128)(2,1)S(1)} %maximum_select_fusion.1), channel_id=1, source_target_pairs={{0,16},{16,0},{1,17},{17,1},{2,18},{18,2},{3,19},{19,3},{4,20},{20... | collective-permute-start | bytes 1572872 | tf_op jit(solution)/shard_map/cond/branch_0_fun/ppermute | solution.py:171
  104.0 32.7 %copy-start.6 = (f32[1,2048]{1,0:T(1,128)S(1)}, f32[1,2048]{1,0:T(1,128)}, u32[]{:S(2)}) copy-start(f32[1,2048]{1,0:T(1,128)} %param.13) | copy-start | bytes 24580
  104.3 19.2 %collective-permute-start.12 = (bf16[64,2048]{1,0:T(8,128)(2,1)S(1)}, bf16[64,2048]{1,0:T(8,128)(2,1)S(1)}, u32[]{:S(2)}, u32[]{:S(2)}) collective-permute-start(bf16[64,2048]{1,0:T(8,128)(2,1)S(1)} %get-tuple-element.79), channel_id=1, source_target_pairs={{0,4},{4,8},{8,12},{1,5},{5,9},{9,13},{2,6},{6,10},{10,14},{3,7},{... | collective-permute-start | bytes 786440 | tf_op jit(solution)/shard_map/ppermute | solution.py:141
  108.8 16.7 %collective-permute-start.13 = (bf16[64,2048]{1,0:T(8,128)(2,1)S(1)}, bf16[64,2048]{1,0:T(8,128)(2,1)}, u32[]{:S(2)}, u32[]{:S(2)}) collective-permute-start(bf16[64,2048]{1,0:T(8,128)(2,1)S(1)} %get-tuple-element.84), channel_id=1, source_target_pairs={{4,0},{8,4},{12,8},{5,1},{9,5},{13,9},{6,2},{10,6},{14,10},{7,3},{... | collective-permute-start | bytes 786440 | tf_op jit(solution)/shard_map/ppermute | solution.py:141
  110.1 15.4 %collective-permute-start.14 = (bf16[64,2048]{1,0:T(8,128)(2,1)S(1)}, bf16[64,2048]{1,0:T(8,128)(2,1)}, u32[]{:S(2)}, u32[]{:S(2)}) collective-permute-start(bf16[64,2048]{1,0:T(8,128)(2,1)S(1)} %get-tuple-element.83), channel_id=1, source_target_pairs={{0,8},{4,12},{1,9},{5,13},{2,10},{6,14},{3,11},{7,15},{16,24},{20,... | collective-permute-start | bytes 786440 | tf_op jit(solution)/shard_map/ppermute | solution.py:141
  114.8 21.9 %collective-permute-start.15 = (bf16[64,2048]{1,0:T(8,128)(2,1)S(1)}, bf16[64,2048]{1,0:T(8,128)(2,1)}, u32[]{:S(2)}, u32[]{:S(2)}) collective-permute-start(bf16[64,2048]{1,0:T(8,128)(2,1)S(1)} %get-tuple-element.82), channel_id=1, source_target_pairs={{8,0},{12,4},{9,1},{13,5},{10,2},{14,6},{11,3},{15,7},{24,16},{28,... | collective-permute-start | bytes 786440 | tf_op jit(solution)/shard_map/ppermute | solution.py:141
  116.1 20.6 %collective-permute-start.16 = (bf16[64,2048]{1,0:T(8,128)(2,1)S(1)}, bf16[64,2048]{1,0:T(8,128)(2,1)}, u32[]{:S(2)}, u32[]{:S(2)}) collective-permute-start(bf16[64,2048]{1,0:T(8,128)(2,1)S(1)} %get-tuple-element.81), channel_id=1, source_target_pairs={{0,12},{1,13},{2,14},{3,15},{16,28},{17,29},{18,30},{19,31}} | collective-permute-start | bytes 786440 | tf_op jit(solution)/shard_map/ppermute | solution.py:141
  123.5 0.7 copy-start.5
  124.2 12.5 %collective-permute-start.17 = (bf16[64,2048]{1,0:T(8,128)(2,1)S(1)}, bf16[64,2048]{1,0:T(8,128)(2,1)}, u32[]{:S(2)}, u32[]{:S(2)}) collective-permute-start(bf16[64,2048]{1,0:T(8,128)(2,1)S(1)} %get-tuple-element.80), channel_id=1, source_target_pairs={{12,0},{13,1},{14,2},{15,3},{28,16},{29,17},{30,18},{31,19}} | collective-permute-start | bytes 786440 | tf_op jit(solution)/shard_map/ppermute | solution.py:141
Sparse Core Ops, SparseCore 0:
  8.9 30.6 all-gather.1

commit v7 on v6

--- a/solution.py
+++ b/solution.py
@@ -129,18 +129,19 @@
 
 def line_reduce_scatter(x, axis, wire):
     n = lax.axis_size(axis)
-    if n > LINE_MAX:
+    if n > LINE_MAX or n & (n - 1):
         return lax.psum_scatter(x, axis, scatter_dimension=0, tiled=True)
     me = lax.axis_index(axis)
-    chunks = x.reshape((n, x.shape[0] // n) + x.shape[1:])
-    acc = lax.dynamic_index_in_dim(chunks, me, keepdims=False)
-    for k in range(1, n):
-        for rightward in (True, False):
-            dest = jnp.clip(me + k if rightward else me - k, 0, n - 1)
-            sent = lax.dynamic_index_in_dim(chunks, dest, keepdims=False).astype(wire)
-            got = lax.ppermute(sent, axis, line_pairs(n, k, rightward))
-            acc = acc + got.astype(x.dtype)
-    return acc
+    rows = x.shape[0] // n
+    bits = n.bit_length() - 1
+    x = x.reshape((2,) * bits + (rows,) + x.shape[1:])
+    for j in range(bits):
+        level = 1 << j
+        bit = (me // level) % 2
+        keep = lax.dynamic_index_in_dim(x, bit, axis=bits - 1 - j, keepdims=False)
+        send = lax.dynamic_index_in_dim(x, 1 - bit, axis=bits - 1 - j, keepdims=False).astype(wire)
+        x = keep + lax.ppermute(send, axis, [(i, i ^ level) for i in range(n)]).astype(keep.dtype)
+    return x
 
 
 def halving_steps():
@@ -184,10 +185,8 @@
     most = min(active_blocks.shape[1], blocks_local)
     first_block = lax.axis_index("latent") * blocks_local
 
-    def middle(slots):
-        picked_valid, count, flat_order, flat_blocks = slot_table(
-            active_blocks, block_counts, first_block, blocks_local, slots
-        )
+    def middle(slots, table):
+        picked_valid, count, flat_order, flat_blocks = table
         pairs = tiles * slots
         compact = sparse_call(
             encode_kernel,
@@ -225,9 +224,11 @@
             [jnp.sum((listed & (shard_of == s)).astype(jnp.int32), axis=1) for s in range(lax.axis_size("latent"))]
         )
         branch = (jnp.max(per_shard) > FEW).astype(jnp.int32)
-        partial = lax.switch(branch, [lambda: middle(FEW), lambda: middle(most)])
+        few_table = slot_table(active_blocks, block_counts, first_block, blocks_local, FEW)
+        most_table = slot_table(active_blocks, block_counts, first_block, blocks_local, most)
+        partial = lax.switch(branch, [lambda: middle(FEW, few_table), lambda: middle(most, most_table)])
     else:
-        partial = middle(most)
+        partial = middle(most, slot_table(active_blocks, block_counts, first_block, blocks_local, most))
     rebuilt = line_reduce_scatter(partial, "latent", jnp.bfloat16)
     return (rebuilt + dec_bias).astype(jnp.bfloat16)[None]
 

time: 146 us -> 140 us (0.959)
  starting transfers between devices: 26.8 us -> 12.6 us
  waiting for transfers between devices: 68.2 us -> 75.5 us
  Pallas kernels: 14.3 us -> 12.4 us
  other arithmetic: 13.1 us -> 14.8 us
    ppermute x6 -> x2, waiting for transfers between devices: 11.2 us -> 26.7 us  [line_reduce_scatter(): lax.ppermute(send, axis, [(i, i ^ level) for i in range(n)])]
    ppermute x6 -> x2, starting transfers between devices: 20.5 us -> 6.31 us  [line_reduce_scatter(): lax.ppermute(send, axis, [(i, i ^ level) for i in range(n)])]
    all_gather x1, waiting for transfers between devices: 26.2 us -> 18.2 us  [shards(): tokens_all = lax.all_gather(acts, 'latent', axis=1, tiled=True)[0]]
    sort x1 -> x2, other arithmetic: 1.69 us -> 3.8 us  [slot_table(): jnp.argsort(jnp.logical_not(flat_valid).astype(jnp.int32), stable=True)]
    pallas_call x2, Pallas kernels: 14.3 us -> 12.4 us  [sparse_call(): pl.pallas_call(kernel, out_shape=out_shape, in_specs=[smem, smem, smem, p...]
    broadcast_in_dim x1, other arithmetic: 2.32 us -> 0.77 us  [shards(): return (rebuilt + dec_bias).astype(jnp.bfloat16)[None]]
  transfers between devices with their start and end apart: 13 -> 9, of which waited for: 8 -> 9; matrix products, arithmetic and copies ran while one was open for 3% -> 9% of each run, Pallas kernels for 0% -> 0%
where the time goes in v7:
time: 140 us; the launch traced here: 139 us
  waiting for transfers between devices  75.5 us (54%)
  between operations  16 us (11%)
  other arithmetic  14.8 us (11%)
  starting transfers between devices  12.6 us (9%)
  Pallas kernels  12.4 us (9%)
  local copies, waits for them, and re-layouts  7.93 us (6%)
    ppermute x2, waiting for transfers between devices, line_reduce_scatter(): lax.ppermute(send, axis, [(i, i ^ level) for i in range(n)])  26.7 us
    ppermute x3, waiting for transfers between devices, halving_sum(): x = keep + lax.ppermute(send, axis, perm)  19.6 us
    all_gather x1, waiting for transfers between devices, shards(): tokens_all = lax.all_gather(acts, 'latent', axis=1, tiled=True)[0]  18.2 us
    pallas_call x2, Pallas kernels, sparse_call(): pl.pallas_call(kernel, out_shape=out_shape, in_specs=[smem, smem, smem, p...  12.4 us
    ppermute x3, waiting for transfers between devices, doubling_gather(): got = lax.ppermute(x, axis, perm)  10.3 us
    ppermute x2, starting transfers between devices, line_reduce_scatter(): lax.ppermute(send, axis, [(i, i ^ level) for i in range(n)])  6.31 us
    sort x2, other arithmetic, slot_table(): jnp.argsort(jnp.logical_not(flat_valid).astype(jnp.int32), stable=True)  3.8 us
    ppermute x3, starting transfers between devices, doubling_gather(): got = lax.ppermute(x, axis, perm)  3.13 us
  transfers between devices with their start and end apart: 9, of which 9 were waited for; matrix products, arithmetic and copies ran while one was open for 9% of the time, Pallas kernels for 0%

profile of v7, /device:TPU:0, one launch (start us, length us, event | category | flops | bytes accessed | tf_op | source)
XLA Modules:
  0.0 139.4 jit_solution(3472037933957620633)
XLA Ops:
  7.3 0.8 not_convert_fusion.2
  8.1 0.8 sort.53
  8.9 0.9 fusion.12
  15.3 0.7 gather_fusion.6
  16.5 0.9 gather_fusion.7
  17.6 1.7 %sort.54 = (s32[32]{0:T(128)}, s32[32]{0:T(128)S(1)}) sort(s32[32]{0:T(128)S(1)} %get-tuple-element.159, s32[32]{0:T(128)S(1)} %iota.24), dimensions={0}, to_apply=%region_9.10 | sort | flops 160 | bytes 512 | tf_op jit(solution)/shard_map/jit(argsort)/sort | solution.py:23
  19.3 2.1 %sort.55 = (s32[64]{0:T(128)}, s32[64]{0:T(128)S(1)}) sort(s32[64]{0:T(128)S(1)} %get-tuple-element.155, s32[64]{0:T(128)S(1)} %iota.25), dimensions={0}, to_apply=%region_10.11 | sort | flops 384 | bytes 1024 | tf_op jit(solution)/shard_map/jit(argsort)/sort | solution.py:23
  21.4 18.2 %all-gather.2.cloned.1.call-done = bf16[1,256,2048]{2,1,0:T(8,128)(2,1)} async-done(((bf16[1,64,2048]{2,1,0:T(8,128)(2,1)}), bf16[1,256,2048]{2,1,0:T(8,128)(2,1)}) %all-gather.2.cloned.1.call-update) | async-done | bytes 1048592 | tf_op jit(solution)/shard_map/all_gather | solution.py:181
  39.6 57.9 %conditional.1 = (f32[2,2,64,2048]{3,2,1,0:T(8,128)S(1)}) conditional(s32[]{:T(128)} %clamp.3, (s32[2,16]{0,1:T(8,128)S(1)}, s32[2,32]{1,0:T(2,128)S(1)}, s32[2,16,1]{1,0,2:T(2,128)S(1)}, pred[32]{0:T(512)(128)(4,1)S(1)}, pred[32]{0:T(512)(128)(4,1)S(1)}, /*index=5*/s32[32]{0:T(128)S(1)}, pred[2,16]{0,1:T(8,128)(4,1)S(1)}, ...), branch_computations={%region_11.14_spmd, %region_14.17_spmd} | conditional | flops 8607893504 | bytes 123191752 | solution.py:229
  40.3 0.8 gather_fusion.2
  41.1 1.2 gather_fusion
  42.3 6.6 %branch_0_fun.2 = f32[2,16,128,128]{3,2,1,0:T(8,128)} custom-call(s32[1]{0:T(128)} %bitcast.n_ref, s32[32]{0:T(128)S(1)} %get-tuple-element.110.slot_ref, s32[32]{0:T(128)} %gather_fusion, bf16[256,2048]{1,0:T(8,128)(2,1)S(1)} %copy-done.3, bf16[2048,8192]{1,0:T(8,128)(2,1)} %get-tuple-element.118.enc_hbm), custom_call_target="tpu_custom_call" | custom-call | flops 2147483648 | bytes 18874368 | tf_op jit(solution)/shard_map/cond/branch_0_fun/pallas_call | solution.py:91
  48.9 1.5 %constant_dynamic-slice_fusion.2 = f32[2,16,64,128]{3,2,1,0:T(8,128)S(1)} fusion(f32[2,16,128,128]{3,2,1,0:T(8,128)} %branch_0_fun.2, s32[]{:T(128)S(6)} %select_n.209), kind=kLoop, calls=%fused_computation.22 | loop fusion | bytes 2097156 | tf_op jit(solution)/shard_map/cond/branch_0_fun/dynamic_slice | solution.py:165
  50.5 2.7 %collective-permute-done = f32[2,16,64,128]{3,2,1,0:T(8,128)} collective-permute-done((f32[2,16,64,128]{3,2,1,0:T(8,128)S(1)}, f32[2,16,64,128]{3,2,1,0:T(8,128)}, u32[]{:S(2)}, u32[]{:S(2)}) %collective-permute-start) | collective-permute-done | bytes 1048608 | tf_op jit(solution)/shard_map/cond/branch_0_fun/ppermute | solution.py:166
  53.2 1.4 %dynamic-slice_add_fusion = f32[2,16,64,128]{3,2,1,0:T(8,128)S(1)} fusion(f32[2,16,64,128]{3,2,1,0:T(8,128)} %collective-permute-done, f32[2,16,128,128]{3,2,1,0:T(8,128)S(1)} %copy-done, s32[]{:T(128)S(6)} %select_n.208), kind=kLoop, calls=%fused_computation.11 | loop fusion | flops 262144 | bytes 3145732 | tf_op jit(solution)/shard_map/cond/branch_0_fun/add | solution.py:166
  54.7 1.5 %collective-permute-start.1 = (f32[2,16,32,128]{3,2,1,0:T(8,128)S(1)}, f32[2,16,32,128]{3,2,1,0:T(8,128)S(1)}, u32[]{:S(2)}, u32[]{:S(2)}) collective-permute-start(f32[2,16,32,128]{3,2,1,0:T(8,128)S(1)} %constant_dynamic-slice_fusion.1), channel_id=1, source_target_pairs={{0,2},{1,3},{2,0},{3,1},{4,6},{5,7},{6,4},{7,5},{8,10},{9,11},{10,... | collective-permute-start | bytes 1572872 | tf_op jit(solution)/shard_map/cond/branch_0_fun/ppermute | solution.py:166
  56.2 0.8 scatter_custom_fusion
  57.2 11.6 %collective-permute-done.1 = f32[2,16,32,128]{3,2,1,0:T(8,128)S(1)} collective-permute-done((f32[2,16,32,128]{3,2,1,0:T(8,128)S(1)}, f32[2,16,32,128]{3,2,1,0:T(8,128)S(1)}, u32[]{:S(2)}, u32[]{:S(2)}) %collective-permute-start.1) | collective-permute-done | bytes 524320 | tf_op jit(solution)/shard_map/cond/branch_0_fun/ppermute | solution.py:166
  68.9 1.6 %collective-permute-start.2 = (f32[2,16,16,128]{3,2,1,0:T(8,128)S(1)}, f32[2,16,16,128]{3,2,1,0:T(8,128)S(1)}, u32[]{:S(2)}, u32[]{:S(2)}) collective-permute-start(f32[2,16,16,128]{3,2,1,0:T(8,128)S(1)} %constant_dynamic-slice_fusion), channel_id=1, source_target_pairs={{0,1},{1,0},{2,3},{3,2},{4,5},{5,4},{6,7},{7,6},{8,9},{9,8},{10,11... | collective-permute-start | bytes 786440 | tf_op jit(solution)/shard_map/cond/branch_0_fun/ppermute | solution.py:166
  71.1 5.3 %collective-permute-done.2 = f32[2,16,16,128]{3,2,1,0:T(8,128)S(1)} collective-permute-done((f32[2,16,16,128]{3,2,1,0:T(8,128)S(1)}, f32[2,16,16,128]{3,2,1,0:T(8,128)S(1)}, u32[]{:S(2)}, u32[]{:S(2)}) %collective-permute-start.2) | collective-permute-done | bytes 262176 | tf_op jit(solution)/shard_map/cond/branch_0_fun/ppermute | solution.py:166
  76.6 1.6 %collective-permute-start.3 = (bf16[2,16,16,128]{3,2,1,0:T(8,128)(2,1)S(1)}, bf16[2,16,16,128]{3,2,1,0:T(8,128)(2,1)S(1)}, u32[]{:S(2)}, u32[]{:S(2)}) collective-permute-start(bf16[2,16,16,128]{3,2,1,0:T(8,128)(2,1)S(1)} %select_convert_fusion), channel_id=1, source_target_pairs={{0,1},{1,0},{2,3},{3,2},{4,5},{5,4},{6,7},{7,6},{8,9},{9,8},{10,11... | collective-permute-start | bytes 393224 | tf_op jit(solution)/shard_map/cond/branch_0_fun/ppermute | solution.py:172
  78.1 3.5 %collective-permute-done.3 = bf16[2,16,16,128]{3,2,1,0:T(8,128)(2,1)S(1)} collective-permute-done((bf16[2,16,16,128]{3,2,1,0:T(8,128)(2,1)S(1)}, bf16[2,16,16,128]{3,2,1,0:T(8,128)(2,1)S(1)}, u32[]{:S(2)}, u32[]{:S(2)}) %collective-permute-start.3) | collective-permute-done | bytes 131104 | tf_op jit(solution)/shard_map/cond/branch_0_fun/ppermute | solution.py:172
  81.7 1.5 %collective-permute-start.4 = (bf16[2,16,32,128]{3,2,1,0:T(8,128)(2,1)S(1)}, bf16[2,16,32,128]{3,2,1,0:T(8,128)(2,1)S(1)}, u32[]{:S(2)}, u32[]{:S(2)}) collective-permute-start(bf16[2,16,32,128]{3,2,1,0:T(8,128)(2,1)S(1)} %maximum_select_fusion.2), channel_id=1, source_target_pairs={{0,2},{1,3},{2,0},{3,1},{4,6},{5,7},{6,4},{7,5},{8,10},{9,11},{10,... | collective-permute-start | bytes 786440 | tf_op jit(solution)/shard_map/cond/branch_0_fun/ppermute | solution.py:172
  83.2 4.9 %collective-permute-done.4 = bf16[2,16,32,128]{3,2,1,0:T(8,128)(2,1)S(1)} collective-permute-done((bf16[2,16,32,128]{3,2,1,0:T(8,128)(2,1)S(1)}, bf16[2,16,32,128]{3,2,1,0:T(8,128)(2,1)S(1)}, u32[]{:S(2)}, u32[]{:S(2)}) %collective-permute-start.4) | collective-permute-done | bytes 262176 | tf_op jit(solution)/shard_map/cond/branch_0_fun/ppermute | solution.py:172
  88.4 1.9 %collective-permute-done.5 = bf16[2,16,64,128]{3,2,1,0:T(8,128)(2,1)S(1)} collective-permute-done((bf16[2,16,64,128]{3,2,1,0:T(8,128)(2,1)S(1)}, bf16[2,16,64,128]{3,2,1,0:T(8,128)(2,1)S(1)}, u32[]{:S(2)}, u32[]{:S(2)}) %collective-permute-start.5) | collective-permute-done | bytes 524320 | tf_op jit(solution)/shard_map/cond/branch_0_fun/ppermute | solution.py:172
  90.3 1.4 maximum_select_fusion.codes_ref
  91.7 5.8 %branch_0_fun.3 = f32[256,2048]{1,0:T(8,128)S(1)} custom-call(s32[1]{0:T(128)} %bitcast.n_ref, s32[32]{0:T(128)S(1)} %get-tuple-element.110.slot_ref, s32[32]{0:T(128)} %gather_fusion, bf16[2,16,128,128]{3,2,1,0:T(8,128)(2,1)} %maximum_select_fusion.codes_ref, bf16[8192,2048]{1,0:T(8,128)(2,1)} %get-tuple-element.120.dec_hbm), custom_call_target="tpu_custom_call" | custom-call | flops 2147483648 | bytes 16777216 | tf_op jit(solution)/shard_map/cond/branch_0_fun/pallas_call | solution.py:91
  97.6 6.2 %collective-permute-start.12 = (bf16[2,64,2048]{2,1,0:T(8,128)(2,1)S(1)}, bf16[2,64,2048]{2,1,0:T(8,128)(2,1)}, u32[]{:S(2)}, u32[]{:S(2)}) collective-permute-start(bf16[2,64,2048]{2,1,0:T(8,128)(2,1)S(1)} %fusion.4), channel_id=1, source_target_pairs={{0,4},{4,0},{8,12},{12,8},{1,5},{5,1},{9,13},{13,9},{2,6},{6,2},{1... | collective-permute-start | bytes 1572872 | tf_op jit(solution)/shard_map/ppermute | solution.py:143
  103.8 12.3 %collective-permute-done.12 = bf16[2,64,2048]{2,1,0:T(8,128)(2,1)} collective-permute-done((bf16[2,64,2048]{2,1,0:T(8,128)(2,1)S(1)}, bf16[2,64,2048]{2,1,0:T(8,128)(2,1)}, u32[]{:S(2)}, u32[]{:S(2)}) %collective-permute-start.12) | collective-permute-done | bytes 524320 | tf_op jit(solution)/shard_map/ppermute | solution.py:143
  116.1 1.2 bitcast_add_fusion
  117.4 14.3 %collective-permute-done.13 = bf16[64,2048]{1,0:T(8,128)(2,1)S(1)} collective-permute-done((bf16[64,2048]{1,0:T(8,128)(2,1)S(1)}, bf16[64,2048]{1,0:T(8,128)(2,1)S(1)}, u32[]{:S(2)}, u32[]{:S(2)}) %collective-permute-start.13) | collective-permute-done | bytes 262176 | tf_op jit(solution)/shard_map/ppermute | solution.py:143
  131.8 0.8 fusion.8
  (59 shorter events, 6.8 us)
Async XLA Ops:
  6.5 33.0 %all-gather.2.cloned.1.call-start = ((), (), s32[]{:S(2)}) async-start(), calls=%async_computation | async-start | bytes 1310720 | tf_op jit(solution)/shard_map/all_gather | solution.py:181
  39.6 2.7 %copy-start.3 = (bf16[256,2048]{1,0:T(8,128)(2,1)S(1)}, bf16[256,2048]{1,0:T(8,128)(2,1)}, u32[]{:S(2)}) copy-start(bf16[256,2048]{1,0:T(8,128)(2,1)} %get-tuple-element.117.acts_ref) | copy-start | bytes 3145732 | tf_op jit(solution)/shard_map/cond
  48.9 4.3 %copy-start = (f32[2,16,128,128]{3,2,1,0:T(8,128)S(1)}, f32[2,16,128,128]{3,2,1,0:T(8,128)}, u32[]{:S(2)}) copy-start(f32[2,16,128,128]{3,2,1,0:T(8,128)} %branch_0_fun.2) | copy-start | bytes 6291460 | tf_op jit(solution)/shard_map/cond
  50.4 2.9 %collective-permute-start = (f32[2,16,64,128]{3,2,1,0:T(8,128)S(1)}, f32[2,16,64,128]{3,2,1,0:T(8,128)}, u32[]{:S(2)}, u32[]{:S(2)}) collective-permute-start(f32[2,16,64,128]{3,2,1,0:T(8,128)S(1)} %constant_dynamic-slice_fusion.2), channel_id=1, source_target_pairs={{0,16},{16,0},{1,17},{17,1},{2,18},{18,2},{3,19},{19,3},{4,20},{20... | collective-permute-start | bytes 3145736 | tf_op jit(solution)/shard_map/cond/branch_0_fun/ppermute | solution.py:166
  54.7 15.9 %copy-start.1 = (f32[8192]{0:T(1024)S(1)}, f32[8192]{0:T(1024)}, u32[]{:S(2)}) copy-start(f32[8192]{0:T(1024)} %get-tuple-element.119) | copy-start | bytes 98308 | tf_op jit(solution)/shard_map/cond
  54.7 14.0 %collective-permute-start.1 = (f32[2,16,32,128]{3,2,1,0:T(8,128)S(1)}, f32[2,16,32,128]{3,2,1,0:T(8,128)S(1)}, u32[]{:S(2)}, u32[]{:S(2)}) collective-permute-start(f32[2,16,32,128]{3,2,1,0:T(8,128)S(1)} %constant_dynamic-slice_fusion.1), channel_id=1, source_target_pairs={{0,2},{1,3},{2,0},{3,1},{4,6},{5,7},{6,4},{7,5},{8,10},{9,11},{10,... | collective-permute-start | bytes 1572872 | tf_op jit(solution)/shard_map/cond/branch_0_fun/ppermute | solution.py:166
  68.9 7.6 %collective-permute-start.2 = (f32[2,16,16,128]{3,2,1,0:T(8,128)S(1)}, f32[2,16,16,128]{3,2,1,0:T(8,128)S(1)}, u32[]{:S(2)}, u32[]{:S(2)}) collective-permute-start(f32[2,16,16,128]{3,2,1,0:T(8,128)S(1)} %constant_dynamic-slice_fusion), channel_id=1, source_target_pairs={{0,1},{1,0},{2,3},{3,2},{4,5},{5,4},{6,7},{7,6},{8,9},{9,8},{10,11... | collective-permute-start | bytes 786440 | tf_op jit(solution)/shard_map/cond/branch_0_fun/ppermute | solution.py:166
  76.6 5.0 %collective-permute-start.3 = (bf16[2,16,16,128]{3,2,1,0:T(8,128)(2,1)S(1)}, bf16[2,16,16,128]{3,2,1,0:T(8,128)(2,1)S(1)}, u32[]{:S(2)}, u32[]{:S(2)}) collective-permute-start(bf16[2,16,16,128]{3,2,1,0:T(8,128)(2,1)S(1)} %select_convert_fusion), channel_id=1, source_target_pairs={{0,1},{1,0},{2,3},{3,2},{4,5},{5,4},{6,7},{7,6},{8,9},{9,8},{10,11... | collective-permute-start | bytes 393224 | tf_op jit(solution)/shard_map/cond/branch_0_fun/ppermute | solution.py:172
  81.7 6.4 %collective-permute-start.4 = (bf16[2,16,32,128]{3,2,1,0:T(8,128)(2,1)S(1)}, bf16[2,16,32,128]{3,2,1,0:T(8,128)(2,1)S(1)}, u32[]{:S(2)}, u32[]{:S(2)}) collective-permute-start(bf16[2,16,32,128]{3,2,1,0:T(8,128)(2,1)S(1)} %maximum_select_fusion.2), channel_id=1, source_target_pairs={{0,2},{1,3},{2,0},{3,1},{4,6},{5,7},{6,4},{7,5},{8,10},{9,11},{10,... | collective-permute-start | bytes 786440 | tf_op jit(solution)/shard_map/cond/branch_0_fun/ppermute | solution.py:172
  88.3 2.0 %collective-permute-start.5 = (bf16[2,16,64,128]{3,2,1,0:T(8,128)(2,1)S(1)}, bf16[2,16,64,128]{3,2,1,0:T(8,128)(2,1)S(1)}, u32[]{:S(2)}, u32[]{:S(2)}) collective-permute-start(bf16[2,16,64,128]{3,2,1,0:T(8,128)(2,1)S(1)} %maximum_select_fusion.1), channel_id=1, source_target_pairs={{0,16},{16,0},{1,17},{17,1},{2,18},{18,2},{3,19},{19,3},{4,20},{20... | collective-permute-start | bytes 1572872 | tf_op jit(solution)/shard_map/cond/branch_0_fun/ppermute | solution.py:172
  97.5 34.3 %copy-start.5 = (f32[1,2048]{1,0:T(1,128)S(1)}, f32[1,2048]{1,0:T(1,128)}, u32[]{:S(2)}) copy-start(f32[1,2048]{1,0:T(1,128)} %param.13) | copy-start | bytes 24580
  97.6 18.6 %collective-permute-start.12 = (bf16[2,64,2048]{2,1,0:T(8,128)(2,1)S(1)}, bf16[2,64,2048]{2,1,0:T(8,128)(2,1)}, u32[]{:S(2)}, u32[]{:S(2)}) collective-permute-start(bf16[2,64,2048]{2,1,0:T(8,128)(2,1)S(1)} %fusion.4), channel_id=1, source_target_pairs={{0,4},{4,0},{8,12},{12,8},{1,5},{5,1},{9,13},{13,9},{2,6},{6,2},{1... | collective-permute-start | bytes 1572872 | tf_op jit(solution)/shard_map/ppermute | solution.py:143
  117.4 14.4 %collective-permute-start.13 = (bf16[64,2048]{1,0:T(8,128)(2,1)S(1)}, bf16[64,2048]{1,0:T(8,128)(2,1)S(1)}, u32[]{:S(2)}, u32[]{:S(2)}) collective-permute-start(bf16[64,2048]{1,0:T(8,128)(2,1)S(1)} %fusion.7), channel_id=1, source_target_pairs={{0,8},{4,12},{8,0},{12,4},{1,9},{5,13},{9,1},{13,5},{2,10},{6,14},... | collective-permute-start | bytes 786440 | tf_op jit(solution)/shard_map/ppermute | solution.py:143
Sparse Core Ops, SparseCore 0:
  8.9 30.6 all-gather.1

commit v8 on v7

v8 whole, which is shorter than its diff:
```python
import functools

import jax
import jax.numpy as jnp
from jax import lax
from jax.experimental import pallas as pl
from jax.experimental.pallas import tpu as pltpu
from jax.sharding import PartitionSpec as P

BLOCK = 128
TILE = 128


def pair_table(active_blocks, block_counts, first_block, blocks_local, capacity):
    tiles, listed = active_blocks.shape
    slot_ids = jnp.arange(listed, dtype=jnp.int32)
    local = active_blocks - first_block
    valid = ((slot_ids[None, :] < block_counts[:, None]) & (local >= 0) & (local < blocks_local)).reshape(-1)
    order = jnp.argsort(jnp.logical_not(valid).astype(jnp.int32), stable=True)[:capacity].astype(jnp.int32)
    pair_valid = valid[order]
    pair_tile = order // listed
    pair_block = jnp.where(pair_valid, local.reshape(-1)[order], 0)
    count = jnp.minimum(jnp.sum(valid.astype(jnp.int32)), capacity).reshape(1)
    return pair_valid, count, pair_tile, pair_block


DEPTH = 6


def weight_stream(n, blk_ref, source, buf, sem, compute):
    def copy(i, slot):
        return pltpu.make_async_copy(source(blk_ref[i]), buf.at[slot], sem.at[slot])

    for j in range(DEPTH):
        @pl.when(j < n)
        def _():
            copy(j, j).start()

    def body(i, carry):
        slot = i % DEPTH
        copy(i, slot).wait()
        compute(i, buf.at[slot])

        @pl.when(i + DEPTH < n)
        def _():
            copy(i + DEPTH, slot).start()

        return carry

    lax.fori_loop(0, n, body, 0)


def encode_kernel(n_ref, tile_ref, blk_ref, acts_ref, enc_hbm, out_ref, buf, sem):
    out_ref[...] = jnp.zeros(out_ref.shape, out_ref.dtype)

    def source(b):
        return enc_hbm.at[:, pl.ds(pl.multiple_of(b * BLOCK, BLOCK), BLOCK)]

    def compute(i, block):
        rows = acts_ref[pl.ds(pl.multiple_of(tile_ref[i] * TILE, TILE), TILE), :]
        out_ref[i] = jnp.dot(rows, block[...], preferred_element_type=jnp.float32)

    weight_stream(n_ref[0], blk_ref, source, buf, sem, compute)


def decode_kernel(n_ref, tile_ref, blk_ref, codes_ref, dec_hbm, out_ref, buf, sem):
    out_ref[...] = jnp.zeros(out_ref.shape, out_ref.dtype)

    def source(b):
        return dec_hbm.at[pl.ds(pl.multiple_of(b * BLOCK, BLOCK), BLOCK), :]

    def compute(i, block):
        rows = pl.ds(pl.multiple_of(tile_ref[i] * TILE, TILE), TILE)
        out_ref[rows, :] += jnp.dot(codes_ref[i], block[...], preferred_element_type=jnp.float32)

    weight_stream(n_ref[0], blk_ref, source, buf, sem, compute)


def sparse_call(kernel, out_shape, buf_shape, count, pair_tile, pair_block, dense, weight, flops, nbytes):
    smem = pl.BlockSpec(memory_space=pltpu.SMEM)
    return pl.pallas_call(
        kernel,
        out_shape=out_shape,
        in_specs=[smem, smem, smem, pl.BlockSpec(memory_space=pltpu.VMEM), pl.BlockSpec(memory_space=pl.ANY)],
        out_specs=pl.BlockSpec(memory_space=pltpu.VMEM),
        scratch_shapes=[pltpu.VMEM((DEPTH,) + buf_shape, weight.dtype), pltpu.SemaphoreType.DMA((DEPTH,))],
        cost_estimate=pl.CostEstimate(flops=flops, bytes_accessed=nbytes, transcendentals=0),
    )(count, pair_tile, pair_block, dense, weight)


LINE_MAX = 4
CAPACITIES = (16, 24)


def line_pairs(n, k, rightward):
    return [(i, i + k) if rightward else (i + k, i) for i in range(n - k)]


def line_gather(x, axis):
    n = lax.axis_size(axis)
    if n > LINE_MAX:
        return lax.all_gather(x, axis, axis=0, tiled=True)
    me = lax.axis_index(axis)
    parts = [x]
    sources = [me]
    for k in range(1, n):
        parts.append(lax.ppermute(x, axis, line_pairs(n, k, True)))
        sources.append(me - k)
        parts.append(lax.ppermute(x, axis, line_pairs(n, k, False)))
        sources.append(me + k)
    out = jnp.zeros((n,) + x.shape, x.dtype)
    for part, src in zip(parts, sources):
        ok = (src >= 0) & (src < n)
        out = lax.dynamic_update_index_in_dim(
            out, jnp.where(ok, part, out[jnp.clip(src, 0, n - 1)]), jnp.clip(src, 0, n - 1), 0
        )
    return out.reshape((n * x.shape[0],) + x.shape[1:])


def line_reduce_scatter(x, axis, wire):
    n = lax.axis_size(axis)
    if n > LINE_MAX or n & (n - 1):
        return lax.psum_scatter(x, axis, scatter_dimension=0, tiled=True)
    me = lax.axis_index(axis)
    rows = x.shape[0] // n
    bits = n.bit_length() - 1
    x = x.reshape((2,) * bits + (rows,) + x.shape[1:])
    for j in range(bits):
        level = 1 << j
        bit = (me // level) % 2
        keep = lax.dynamic_index_in_dim(x, bit, axis=bits - 1 - j, keepdims=False)
        send = lax.dynamic_index_in_dim(x, 1 - bit, axis=bits - 1 - j, keepdims=False).astype(wire)
        x = keep + lax.ppermute(send, axis, [(i, i ^ level) for i in range(n)]).astype(keep.dtype)
    return x


def halving_steps():
    steps = []
    for axis in ("section", "tok"):
        n = lax.axis_size(axis)
        if n & (n - 1):
            return None
        me = lax.axis_index(axis)
        level = n // 2
        while level:
            steps.append((axis, (me // level) % 2, [(i, i ^ level) for i in range(n)]))
            level //= 2
    return steps


def halving_sum(x, steps):
    for axis, bit, perm in steps:
        half = x.shape[1] // 2
        keep = lax.dynamic_slice_in_dim(x, bit * half, half, axis=1)
        send = lax.dynamic_slice_in_dim(x, (1 - bit) * half, half, axis=1)
        x = keep + lax.ppermute(send, axis, perm)
    return x


def doubling_gather(x, steps):
    for axis, bit, perm in reversed(steps):
        got = lax.ppermute(x, axis, perm)
        x = jnp.where(bit == 0, jnp.concatenate([x, got], axis=1), jnp.concatenate([got, x], axis=1))
    return x


def shards(acts, enc_weight, enc_bias, dec_weight, dec_bias, active_blocks, block_counts):
    local_enc = enc_weight[0]
    local_dec = dec_weight[:, 0, :]
    width, n_lat = local_enc.shape
    tokens_all = lax.all_gather(acts, "latent", axis=1, tiled=True)[0]
    n_tok = tokens_all.shape[0]
    tiles = n_tok // TILE
    blocks_local = n_lat // BLOCK
    most = tiles * min(active_blocks.shape[1], blocks_local)
    first_block = lax.axis_index("latent") * blocks_local

    def table(capacity):
        return pair_table(active_blocks, block_counts, first_block, blocks_local, capacity)

    def middle(capacity, pairs):
        pair_valid, count, pair_tile, pair_block = pairs
        compact = sparse_call(
            encode_kernel,
            jax.ShapeDtypeStruct((capacity, TILE, BLOCK), jnp.float32),
            (width, BLOCK),
            count, pair_tile, pair_block, tokens_all, local_enc,
            2 * capacity * TILE * width * BLOCK, capacity * (width * BLOCK * 2 + TILE * BLOCK * 4),
        )
        steps = halving_steps()
        if steps is None:
            shared = lax.psum_scatter(compact, ("section", "tok"), scatter_dimension=1, tiled=True)
        else:
            shared = halving_sum(compact, steps)
        bias_pairs = enc_bias.reshape(blocks_local, BLOCK)[pair_block]
        codes_part = jnp.where(
            pair_valid[:, None, None], jax.nn.relu(shared + bias_pairs[:, None, :]), 0.0
        ).astype(jnp.bfloat16)
        if steps is None:
            codes = lax.all_gather(codes_part, ("section", "tok"), axis=1, tiled=True)
        else:
            codes = doubling_gather(codes_part, steps)
        return sparse_call(
            decode_kernel,
            jax.ShapeDtypeStruct((n_tok, local_dec.shape[1]), jnp.float32),
            (BLOCK, local_dec.shape[1]),
            count, pair_tile, pair_block, codes, local_dec,
            2 * capacity * TILE * BLOCK * local_dec.shape[1], capacity * BLOCK * local_dec.shape[1] * 2,
        )

    levels = [c for c in CAPACITIES if c < most]
    if levels:
        listed = jnp.arange(active_blocks.shape[1], dtype=jnp.int32)[None, :] < block_counts[:, None]
        shard_of = active_blocks // blocks_local
        fullest = jnp.max(
            jnp.stack([jnp.sum((listed & (shard_of == s)).astype(jnp.int32)) for s in range(lax.axis_size("latent"))])
        )
        branch = sum((fullest > c).astype(jnp.int32) for c in levels)
        tables = [table(c) for c in levels + [most]]
        partial = lax.switch(branch, [functools.partial(middle, c, t) for c, t in zip(levels + [most], tables)])
    else:
        partial = middle(most, table(most))
    rebuilt = line_reduce_scatter(partial, "latent", jnp.bfloat16)
    return (rebuilt + dec_bias).astype(jnp.bfloat16)[None]


def solution(mesh):
    placed = (
        P("section", "latent", "tok"),
        P("section", "tok", "latent"),
        P("latent"),
        P("latent", "section", "tok"),
        P("section", "tok"),
        P(),
        P(),
    )
    return jax.shard_map(
        shards, mesh=mesh, in_specs=placed, out_specs=P("section", "latent", "tok"), check_vma=False
    )
```

time: 140 us -> 124 us (0.89)
  starting transfers between devices: 12.6 us -> 6.44 us
  local copies, waits for them, and re-layouts: 7.93 us -> 3.31 us
  other arithmetic: 14.8 us -> 10.2 us
  waiting for transfers between devices: 75.5 us -> 72.9 us
  Pallas kernels: 12.4 us -> 14.8 us
    ppermute x3, waiting for transfers between devices: 19.6 us -> 11.7 us  [halving_sum(): x = keep + lax.ppermute(send, axis, perm)]
    all_gather x1, waiting for transfers between devices: 18.2 us -> 24.8 us  [shards(): tokens_all = lax.all_gather(acts, 'latent', axis=1, tiled=True)[0]]
    ppermute x2, starting transfers between devices: 6.31 us -> 0.14 us  [line_reduce_scatter(): lax.ppermute(send, axis, [(i, i ^ level) for i in range(n)])]
    gather x11 -> x3, local copies, waits for them, and re-layouts: 4.68 us -> 1.89 us  [the longest x1 0.66 us: pair_table(): pair_block = jnp.where(pair_valid, local.reshape(-1)[order], 0)]
    reduce_max x4 -> x0, other arithmetic: 2.64 us -> none  [shards(): branch = (jnp.max(per_shard) > FEW).astype(jnp.int32)]
    sort x3 -> x1, other arithmetic: 4.61 us -> 2.01 us  [pair_table(): jnp.argsort(jnp.logical_not(valid).astype(jnp.int32), stable=True)]
    ppermute x3, waiting for transfers between devices: 10.3 us -> 7.8 us  [doubling_gather(): got = lax.ppermute(x, axis, perm)]
    pallas_call x2, Pallas kernels: 12.4 us -> 14.8 us  [sparse_call(): pl.pallas_call(kernel, out_shape=out_shape, in_specs=[smem, smem, smem, p...]
  transfers between devices with their start and end apart: 9 -> 9, of which waited for: 9 -> 9; matrix products, arithmetic and copies ran while one was open for 9% -> 5% of each run, Pallas kernels for 0% -> 0%
where the time goes in v8:
time: 124 us
  waiting for transfers between devices  72.9 us (59%)
  between operations  16 us (13%)
  Pallas kernels  14.8 us (12%)
  other arithmetic  10.2 us (8%)
  starting transfers between devices  6.44 us (5%)
  local copies, waits for them, and re-layouts  3.31 us (3%)
    ppermute x2, waiting for transfers between devices, line_reduce_scatter(): lax.ppermute(send, axis, [(i, i ^ level) for i in range(n)])  28 us
    all_gather x1, waiting for transfers between devices, shards(): tokens_all = lax.all_gather(acts, 'latent', axis=1, tiled=True)[0]  24.8 us
    pallas_call x2, Pallas kernels, sparse_call(): pl.pallas_call(kernel, out_shape=out_shape, in_specs=[smem, smem, smem, p...  14.8 us
    ppermute x3, waiting for transfers between devices, halving_sum(): x = keep + lax.ppermute(send, axis, perm)  11.7 us
    ppermute x3, waiting for transfers between devices, doubling_gather(): got = lax.ppermute(x, axis, perm)  7.8 us
    ppermute x3, starting transfers between devices, doubling_gather(): got = lax.ppermute(x, axis, perm)  3.15 us
    ppermute x3, starting transfers between devices, halving_sum(): x = keep + lax.ppermute(send, axis, perm)  3.14 us
  transfers between devices with their start and end apart: 9, of which 9 were waited for; matrix products, arithmetic and copies ran while one was open for 5% of the time, Pallas kernels for 0%

profile of v8, /device:TPU:0, one launch (start us, length us, event | category | flops | bytes accessed | tf_op | source)
XLA Modules:
  0.0 124.5 jit_solution(9592600479254633569)
XLA Ops:
  6.5 0.7 all-gather.2.cloned.1.call-update
  7.3 1.4 %convert_reduce_fusion = (s32[]{:T(128)}, pred[2,32]{1,0:T(4,128)(4,1)S(1)}, s32[2,32]{1,0:T(2,128)S(1)}, s32[2,32]{1,0:T(2,128)S(1)}) fusion(s32[2]{0:T(128)} %param.16, s32[2,32]{1,0:T(2,128)} %param.15, s32[]{:T(128)S(6)} %mul.57), kind=kLoop, calls=%fused_computation.86 | loop fusion | flops 1471 | bytes 848 | tf_op jit(solution)/shard_map/reduce_sum | solution.py:23
  8.7 1.5 %fusion.8 = (s32[]{:T(128)}, s32[]{:T(128)}, s32[]{:T(128)}, s32[]{:T(128)}) fusion(s32[2,32]{1,0:T(2,128)S(1)} %get-tuple-element.273, s32[2]{0:T(128)} %param.16), kind=kLoop, calls=%fused_computation.85 | loop fusion | flops 1084 | bytes 280 | tf_op jit(solution)/shard_map/reduce_sum | solution.py:216
  12.8 2.0 %sort.21 = (s32[64]{0:T(128)}, s32[64]{0:T(128)S(1)}) sort(s32[64]{0:T(128)S(1)} %not_convert_fusion, s32[64]{0:T(128)S(1)} %iota.13), dimensions={0}, to_apply=%region_5.6 | sort | flops 384 | bytes 1024 | tf_op jit(solution)/shard_map/jit(argsort)/sort | solution.py:19
  14.8 24.8 %all-gather.2.cloned.1.call-done = bf16[1,256,2048]{2,1,0:T(8,128)(2,1)} async-done(((bf16[1,64,2048]{2,1,0:T(8,128)(2,1)}), bf16[1,256,2048]{2,1,0:T(8,128)(2,1)}) %all-gather.2.cloned.1.call-update) | async-done | bytes 1048592 | tf_op jit(solution)/shard_map/all_gather | solution.py:171
  39.6 47.8 %conditional.1 = (f32[2,2,64,2048]{3,2,1,0:T(8,128)S(1)}) conditional(s32[]{:T(128)} %clamp.3, (s32[]{:T(128)}, s32[64]{0:T(128)S(1)}, (), s32[]{:T(128)}, pred[64]{0:T(512)(128)(4,1)S(1)}, /*index=5*/s32[64]{0:T(128)S(1)}, bf16[256,2048]{1,0:T(8,128)(2,1)}, bf16[2048,8192]{1,0:T(8,128)(2,1)}, f32[8192]{0:T(1024)}, ...), branch_computations={%region_6.7_spmd, %region_7.8_spmd, %region_8.9_spmd} | conditional | flops 8607895552 | bytes 118993720 | solution.py:220
  39.6 0.5 compare_select_fusion.1
  40.1 0.7 gather_fusion
  40.8 0.7 gather_fusion.1
  42.1 0.5 compare_select_fusion
  42.7 8.0 %branch_0_fun.2 = f32[16,128,128]{2,1,0:T(8,128)} custom-call(s32[1]{0:T(128)} %bitcast.n_ref, s32[16]{0:T(128)} %get-tuple-element.268.tile_ref, s32[16]{0:T(128)} %get-tuple-element.259.blk_ref, bf16[256,2048]{1,0:T(8,128)(2,1)} %get-tuple-element.217.acts_ref, bf16[2048,8192]{1,0:T(8,128)(2,1)} %get-tuple-element.218.enc_hbm), custom_call_target="tpu_custom_call" | custom-call | flops 1073741824 | bytes 9437184 | tf_op jit(solution)/shard_map/cond/branch_0_fun/pallas_call | solution.py:81
  50.7 1.1 constant_dynamic-slice_fusion.2
  51.9 1.9 %collective-permute-done = f32[16,64,128]{2,1,0:T(8,128)S(1)} collective-permute-done((f32[16,64,128]{2,1,0:T(8,128)S(1)}, f32[16,64,128]{2,1,0:T(8,128)S(1)}, u32[]{:S(2)}, u32[]{:S(2)}) %collective-permute-start) | collective-permute-done | bytes 524320 | tf_op jit(solution)/shard_map/cond/branch_0_fun/ppermute | solution.py:156
  53.8 1.1 dynamic-slice_add_fusion
  54.9 1.5 %collective-permute-start.1 = (f32[16,32,128]{2,1,0:T(8,128)S(1)}, f32[16,32,128]{2,1,0:T(8,128)S(1)}, u32[]{:S(2)}, u32[]{:S(2)}) collective-permute-start(f32[16,32,128]{2,1,0:T(8,128)S(1)} %constant_dynamic-slice_fusion.1), channel_id=1, source_target_pairs={{0,2},{1,3},{2,0},{3,1},{4,6},{5,7},{6,4},{7,5},{8,10},{9,11},{10,... | collective-permute-start | bytes 786440 | tf_op jit(solution)/shard_map/cond/branch_0_fun/ppermute | solution.py:156
  56.4 6.9 %collective-permute-done.1 = f32[16,32,128]{2,1,0:T(8,128)S(1)} collective-permute-done((f32[16,32,128]{2,1,0:T(8,128)S(1)}, f32[16,32,128]{2,1,0:T(8,128)S(1)}, u32[]{:S(2)}, u32[]{:S(2)}) %collective-permute-start.1) | collective-permute-done | bytes 262176 | tf_op jit(solution)/shard_map/cond/branch_0_fun/ppermute | solution.py:156
  63.4 1.5 %collective-permute-start.2 = (f32[16,16,128]{2,1,0:T(8,128)S(1)}, f32[16,16,128]{2,1,0:T(8,128)S(1)}, u32[]{:S(2)}, u32[]{:S(2)}) collective-permute-start(f32[16,16,128]{2,1,0:T(8,128)S(1)} %constant_dynamic-slice_fusion), channel_id=1, source_target_pairs={{0,1},{1,0},{2,3},{3,2},{4,5},{5,4},{6,7},{7,6},{8,9},{9,8},{10,11... | collective-permute-start | bytes 393224 | tf_op jit(solution)/shard_map/cond/branch_0_fun/ppermute | solution.py:156
  64.9 0.6 gather_fusion.2
  65.5 2.9 %collective-permute-done.2 = f32[16,16,128]{2,1,0:T(8,128)S(1)} collective-permute-done((f32[16,16,128]{2,1,0:T(8,128)S(1)}, f32[16,16,128]{2,1,0:T(8,128)S(1)}, u32[]{:S(2)}, u32[]{:S(2)}) %collective-permute-start.2) | collective-permute-done | bytes 131104 | tf_op jit(solution)/shard_map/cond/branch_0_fun/ppermute | solution.py:156
  68.4 0.1 select_convert_fusion
  68.5 1.5 %collective-permute-start.3 = (bf16[16,16,128]{2,1,0:T(8,128)(2,1)S(1)}, bf16[16,16,128]{2,1,0:T(8,128)(2,1)S(1)}, u32[]{:S(2)}, u32[]{:S(2)}) collective-permute-start(bf16[16,16,128]{2,1,0:T(8,128)(2,1)S(1)} %select_convert_fusion), channel_id=1, source_target_pairs={{0,1},{1,0},{2,3},{3,2},{4,5},{5,4},{6,7},{7,6},{8,9},{9,8},{10,11... | collective-permute-start | bytes 196616 | tf_op jit(solution)/shard_map/cond/branch_0_fun/ppermute | solution.py:162
  70.0 2.8 %collective-permute-done.3 = bf16[16,16,128]{2,1,0:T(8,128)(2,1)S(1)} collective-permute-done((bf16[16,16,128]{2,1,0:T(8,128)(2,1)S(1)}, bf16[16,16,128]{2,1,0:T(8,128)(2,1)S(1)}, u32[]{:S(2)}, u32[]{:S(2)}) %collective-permute-start.3) | collective-permute-done | bytes 65568 | tf_op jit(solution)/shard_map/cond/branch_0_fun/ppermute | solution.py:162
  72.9 1.5 %collective-permute-start.4 = (bf16[16,32,128]{2,1,0:T(8,128)(2,1)S(1)}, bf16[16,32,128]{2,1,0:T(8,128)(2,1)S(1)}, u32[]{:S(2)}, u32[]{:S(2)}) collective-permute-start(bf16[16,32,128]{2,1,0:T(8,128)(2,1)S(1)} %maximum_select_fusion.2), channel_id=1, source_target_pairs={{0,2},{1,3},{2,0},{3,1},{4,6},{5,7},{6,4},{7,5},{8,10},{9,11},{10,... | collective-permute-start | bytes 393224 | tf_op jit(solution)/shard_map/cond/branch_0_fun/ppermute | solution.py:162
  74.4 3.5 %collective-permute-done.4 = bf16[16,32,128]{2,1,0:T(8,128)(2,1)S(1)} collective-permute-done((bf16[16,32,128]{2,1,0:T(8,128)(2,1)S(1)}, bf16[16,32,128]{2,1,0:T(8,128)(2,1)S(1)}, u32[]{:S(2)}, u32[]{:S(2)}) %collective-permute-start.4) | collective-permute-done | bytes 131104 | tf_op jit(solution)/shard_map/cond/branch_0_fun/ppermute | solution.py:162
  77.9 0.1 maximum_select_fusion.1
  78.1 1.5 %collective-permute-done.5 = bf16[16,64,128]{2,1,0:T(8,128)(2,1)S(1)} collective-permute-done((bf16[16,64,128]{2,1,0:T(8,128)(2,1)S(1)}, bf16[16,64,128]{2,1,0:T(8,128)(2,1)S(1)}, u32[]{:S(2)}, u32[]{:S(2)}) %collective-permute-start.5) | collective-permute-done | bytes 262176 | tf_op jit(solution)/shard_map/cond/branch_0_fun/ppermute | solution.py:162
  79.6 0.9 maximum_select_fusion.codes_ref
  80.5 6.8 %branch_0_fun.3 = f32[256,2048]{1,0:T(8,128)S(1)} custom-call(s32[1]{0:T(128)} %bitcast.n_ref, s32[16]{0:T(128)} %get-tuple-element.268.tile_ref, s32[16]{0:T(128)} %get-tuple-element.259.blk_ref, bf16[16,128,128]{2,1,0:T(8,128)(2,1)} %maximum_select_fusion.codes_ref, bf16[8192,2048]{1,0:T(8,128)(2,1)} %get-tuple-element.220.dec_hbm), custom_call_target="tpu_custom_call" | custom-call | flops 1073741824 | bytes 8388608 | tf_op jit(solution)/shard_map/cond/branch_0_fun/pallas_call | solution.py:81
  87.6 14.0 %collective-permute-done.18 = bf16[2,64,2048]{2,1,0:T(8,128)(2,1)} collective-permute-done((bf16[2,64,2048]{2,1,0:T(8,128)(2,1)S(1)}, bf16[2,64,2048]{2,1,0:T(8,128)(2,1)}, u32[]{:S(2)}, u32[]{:S(2)}) %collective-permute-start.18) | collective-permute-done | bytes 524320 | tf_op jit(solution)/shard_map/ppermute | solution.py:133
  101.6 1.1 bitcast_add_fusion
  102.9 14.0 %collective-permute-done.19 = bf16[64,2048]{1,0:T(8,128)(2,1)S(1)} collective-permute-done((bf16[64,2048]{1,0:T(8,128)(2,1)S(1)}, bf16[64,2048]{1,0:T(8,128)(2,1)S(1)}, u32[]{:S(2)}, u32[]{:S(2)}) %collective-permute-start.19) | collective-permute-done | bytes 262176 | tf_op jit(solution)/shard_map/ppermute | solution.py:133
  116.9 0.8 fusion.4
  (21 shorter events, 0.7 us)
Async XLA Ops:
  6.5 33.1 %all-gather.2.cloned.1.call-start = ((), (), s32[]{:S(2)}) async-start(), calls=%async_computation | async-start | bytes 1310720 | tf_op jit(solution)/shard_map/all_gather | solution.py:171
  50.7 14.2 %copy-start.1 = (f32[8192]{0:T(1024)S(1)}, f32[8192]{0:T(1024)}, u32[]{:S(2)}) copy-start(f32[8192]{0:T(1024)} %get-tuple-element.219) | copy-start | bytes 98308 | tf_op jit(solution)/shard_map/cond
  51.8 2.0 %collective-permute-start = (f32[16,64,128]{2,1,0:T(8,128)S(1)}, f32[16,64,128]{2,1,0:T(8,128)S(1)}, u32[]{:S(2)}, u32[]{:S(2)}) collective-permute-start(f32[16,64,128]{2,1,0:T(8,128)S(1)} %constant_dynamic-slice_fusion.2), channel_id=1, source_target_pairs={{0,16},{16,0},{1,17},{17,1},{2,18},{18,2},{3,19},{19,3},{4,20},{20... | collective-permute-start | bytes 1572872 | tf_op jit(solution)/shard_map/cond/branch_0_fun/ppermute | solution.py:156
  54.9 8.4 %collective-permute-start.1 = (f32[16,32,128]{2,1,0:T(8,128)S(1)}, f32[16,32,128]{2,1,0:T(8,128)S(1)}, u32[]{:S(2)}, u32[]{:S(2)}) collective-permute-start(f32[16,32,128]{2,1,0:T(8,128)S(1)} %constant_dynamic-slice_fusion.1), channel_id=1, source_target_pairs={{0,2},{1,3},{2,0},{3,1},{4,6},{5,7},{6,4},{7,5},{8,10},{9,11},{10,... | collective-permute-start | bytes 786440 | tf_op jit(solution)/shard_map/cond/branch_0_fun/ppermute | solution.py:156
  63.4 5.0 %collective-permute-start.2 = (f32[16,16,128]{2,1,0:T(8,128)S(1)}, f32[16,16,128]{2,1,0:T(8,128)S(1)}, u32[]{:S(2)}, u32[]{:S(2)}) collective-permute-start(f32[16,16,128]{2,1,0:T(8,128)S(1)} %constant_dynamic-slice_fusion), channel_id=1, source_target_pairs={{0,1},{1,0},{2,3},{3,2},{4,5},{5,4},{6,7},{7,6},{8,9},{9,8},{10,11... | collective-permute-start | bytes 393224 | tf_op jit(solution)/shard_map/cond/branch_0_fun/ppermute | solution.py:156
  68.5 4.3 %collective-permute-start.3 = (bf16[16,16,128]{2,1,0:T(8,128)(2,1)S(1)}, bf16[16,16,128]{2,1,0:T(8,128)(2,1)S(1)}, u32[]{:S(2)}, u32[]{:S(2)}) collective-permute-start(bf16[16,16,128]{2,1,0:T(8,128)(2,1)S(1)} %select_convert_fusion), channel_id=1, source_target_pairs={{0,1},{1,0},{2,3},{3,2},{4,5},{5,4},{6,7},{7,6},{8,9},{9,8},{10,11... | collective-permute-start | bytes 196616 | tf_op jit(solution)/shard_map/cond/branch_0_fun/ppermute | solution.py:162
  72.9 5.0 %collective-permute-start.4 = (bf16[16,32,128]{2,1,0:T(8,128)(2,1)S(1)}, bf16[16,32,128]{2,1,0:T(8,128)(2,1)S(1)}, u32[]{:S(2)}, u32[]{:S(2)}) collective-permute-start(bf16[16,32,128]{2,1,0:T(8,128)(2,1)S(1)} %maximum_select_fusion.2), channel_id=1, source_target_pairs={{0,2},{1,3},{2,0},{3,1},{4,6},{5,7},{6,4},{7,5},{8,10},{9,11},{10,... | collective-permute-start | bytes 393224 | tf_op jit(solution)/shard_map/cond/branch_0_fun/ppermute | solution.py:162
  78.0 1.6 %collective-permute-start.5 = (bf16[16,64,128]{2,1,0:T(8,128)(2,1)S(1)}, bf16[16,64,128]{2,1,0:T(8,128)(2,1)S(1)}, u32[]{:S(2)}, u32[]{:S(2)}) collective-permute-start(bf16[16,64,128]{2,1,0:T(8,128)(2,1)S(1)} %maximum_select_fusion.1), channel_id=1, source_target_pairs={{0,16},{16,0},{1,17},{17,1},{2,18},{18,2},{3,19},{19,3},{4,20},{20... | collective-permute-start | bytes 786440 | tf_op jit(solution)/shard_map/cond/branch_0_fun/ppermute | solution.py:162
  87.4 29.5 %copy-start.4 = (f32[1,2048]{1,0:T(1,128)S(1)}, f32[1,2048]{1,0:T(1,128)}, u32[]{:S(2)}) copy-start(f32[1,2048]{1,0:T(1,128)} %param.14) | copy-start | bytes 24580
  87.5 14.1 %collective-permute-start.18 = (bf16[2,64,2048]{2,1,0:T(8,128)(2,1)S(1)}, bf16[2,64,2048]{2,1,0:T(8,128)(2,1)}, u32[]{:S(2)}, u32[]{:S(2)}) collective-permute-start(bf16[2,64,2048]{2,1,0:T(8,128)(2,1)S(1)} %fusion), channel_id=1, source_target_pairs={{0,4},{4,0},{8,12},{12,8},{1,5},{5,1},{9,13},{13,9},{2,6},{6,2},{1... | collective-permute-start | bytes 1572872 | tf_op jit(solution)/shard_map/ppermute | solution.py:133
  102.8 14.1 %collective-permute-start.19 = (bf16[64,2048]{1,0:T(8,128)(2,1)S(1)}, bf16[64,2048]{1,0:T(8,128)(2,1)S(1)}, u32[]{:S(2)}, u32[]{:S(2)}) collective-permute-start(bf16[64,2048]{1,0:T(8,128)(2,1)S(1)} %fusion.3), channel_id=1, source_target_pairs={{0,8},{4,12},{8,0},{12,4},{1,9},{5,13},{9,1},{13,5},{2,10},{6,14},... | collective-permute-start | bytes 786440 | tf_op jit(solution)/shard_map/ppermute | solution.py:133
Sparse Core Ops, SparseCore 0:
  8.9 30.6 all-gather.1
